TPU v7x, 256 devices: a whole 4x4x8 slice. The times are simulated.
256 devices in a mesh: row: 4 (over y), col: 16 (over z_hi, x, core), dep: 4 (over z_lo).
Axes of the slice: x: 4, y: 4, z: 8 (z_hi: 2, z_lo: 4; z = z_hi * 4 + z_lo), core: 2. Of those that a mesh axis runs over, the one named last changes fastest.
Arguments:
- grad_out: bfloat16 [4, 512, 12288], P('row', 'dep', 'col'), may hold values from -7 to 7
- out_weight: bfloat16 [8192, 12288], P('row', 'col'), may hold values from -0.09375 to 0.09375
- query_rows: bfloat16 [2048, 8192], P('dep', ('row', 'col')), may hold values from -6 to 6
- key_rows: bfloat16 [2048, 8192], P('dep', ('row', 'col')), may hold values from -6 to 6
- value_rows: bfloat16 [2048, 8192], P('dep', ('row', 'col')), may hold values from -7 to 7
- seg_lengths: int32 [8], replicated, may hold values from 1 to 1536, 2048 in all
Outputs:
- grad_weight: float32 [8192, 12288], P('row', 'col')
- grad_query: bfloat16 [2048, 8192], P('dep', ('row', 'col'))
- grad_key: bfloat16 [2048, 8192], P('dep', ('row', 'col'))
- grad_value: bfloat16 [2048, 8192], P('dep', ('row', 'col'))
All inputs are finite; a program needn't handle non-finite values.
Results may differ from a plain program's by a relative error of at most 0.029.
Values may be sent and summed in bfloat16 or wider, within the bound.
No kernel may reach another device: no remote copies, remote signals or barrier semaphores. Data moves between devices by JAX's collectives and lax.ppermute only.
A program may use at most 128 MiB of HBM per device.

v0:
```python
import math

import jax
import jax.numpy as jnp
from jax import lax
from jax.sharding import PartitionSpec as P

NEG_FILL = -1e30


def segment_count(positions, seg_ends):
    return jnp.sum((positions[:, None] >= seg_ends[None, :]).astype(jnp.int32), axis=1)


def shards(grad_out, out_weight, query_rows, key_rows, value_rows, seg_lengths):
    grad_rows = lax.all_gather(grad_out, "row", axis=0, tiled=True).reshape(-1, grad_out.shape[2])
    tok_depth = grad_rows.shape[0]
    head_dim = query_rows.shape[1]
    inv_root = 1.0 / math.sqrt(head_dim)
    context_grad = lax.psum_scatter(
        jnp.einsum("hf,tf->ht", out_weight, grad_rows, preferred_element_type=jnp.float32).astype(
            jnp.bfloat16
        ),
        "col",
        scatter_dimension=0,
        tiled=True,
    )
    keys_all, values_all = (
        lax.all_gather(key_rows, "dep", axis=0, tiled=True),
        lax.all_gather(value_rows, "dep", axis=0, tiled=True),
    )
    key_total = keys_all.shape[0]
    seg_ends = jnp.cumsum(seg_lengths)
    key_pos = jnp.arange(key_total, dtype=jnp.int32)
    key_seg = segment_count(key_pos, seg_ends)
    offset_rows = lax.axis_index("dep") * tok_depth
    block_len = min(512, tok_depth)
    block_count = tok_depth // block_len

    def one_block(block_index, totals):
        context, grad_q, grad_k, grad_v, max_all, sum_all, delta_all = totals
        row_start = block_index * block_len
        query_pos = offset_rows + row_start + jnp.arange(block_len, dtype=jnp.int32)
        query_seg = segment_count(query_pos, seg_ends)
        allowed = (query_seg[:, None] == key_seg[None, :]) & (
            key_pos[None, :] <= query_pos[:, None]
        )
        scores = (
            jnp.einsum("qh,kh->qk", query_rows, keys_all, preferred_element_type=jnp.float32)
            * inv_root
        )
        masked = jnp.where(allowed, scores, NEG_FILL)
        row_max = jnp.max(masked, axis=1, keepdims=True)
        exponent = jnp.where(allowed, jnp.exp(masked - row_max), 0.0)
        row_sum = jnp.sum(exponent, axis=1, keepdims=True)
        prob_full = exponent / row_sum
        prob_half = prob_full.astype(jnp.bfloat16)
        ctx_block = jnp.dot(prob_half, values_all, preferred_element_type=jnp.float32).astype(
            jnp.bfloat16
        )
        grad_prob = jnp.einsum(
            "hq,kh->qk", context_grad, values_all, preferred_element_type=jnp.float32
        )
        delta_row = jnp.sum(prob_full * grad_prob, axis=1, keepdims=True)
        grad_score = (prob_full * (grad_prob - delta_row)).astype(jnp.bfloat16)
        q_grad_block = (
            jnp.dot(grad_score, keys_all, preferred_element_type=jnp.float32) * inv_root
        ).astype(jnp.bfloat16)
        grad_k = grad_k + jnp.einsum(
            "qk,qh->kh", grad_score, query_rows, preferred_element_type=jnp.float32
        )
        grad_v = grad_v + jnp.einsum(
            "qk,hq->kh", prob_half, context_grad, preferred_element_type=jnp.float32
        )
        context = ctx_block
        grad_q = q_grad_block
        max_all = row_max[:, 0]
        sum_all = row_sum[:, 0]
        delta_all = delta_row[:, 0]
        return (context, grad_q, grad_k, grad_v, max_all, sum_all, delta_all)

    start_state = (
        jnp.zeros((tok_depth, head_dim), jnp.bfloat16),
        jnp.zeros((tok_depth, head_dim), jnp.bfloat16),
        jnp.zeros((key_total, head_dim), jnp.float32),
        jnp.zeros((key_total, head_dim), jnp.float32),
        jnp.zeros((tok_depth,), jnp.float32),
        jnp.zeros((tok_depth,), jnp.float32),
        jnp.zeros((tok_depth,), jnp.float32),
    )
    context, grad_query, key_partial, value_partial, max_rows, sum_rows, delta_rows = lax.fori_loop(
        0, block_count, one_block, start_state
    )
    key_sum, value_sum = (
        lax.psum_scatter(
            (key_partial * inv_root).astype(jnp.bfloat16), "dep", scatter_dimension=0, tiled=True
        ).astype(jnp.float32),
        lax.psum_scatter(
            value_partial.astype(jnp.bfloat16), "dep", scatter_dimension=0, tiled=True
        ).astype(jnp.float32),
    )
    grad_key = key_sum.astype(jnp.bfloat16)
    grad_value = value_sum.astype(jnp.bfloat16)
    n_col = lax.axis_size("col")
    n_dep = lax.axis_size("dep")
    everyone = lax.all_gather(context[None], ("col", "dep"), axis=0, tiled=True).reshape(
        n_col, n_dep, tok_depth, head_dim
    )
    depth_grads = lax.all_gather(grad_rows[None], "dep", axis=0, tiled=True)
    grad_weight = jnp.zeros((n_col, head_dim, grad_rows.shape[1]), jnp.float32)
    for depth in range(n_dep):
        piece = jnp.einsum(
            "cth,tf->chf",
            everyone[:, depth],
            depth_grads[depth],
            preferred_element_type=jnp.float32,
        )
        grad_weight = grad_weight + lax.optimization_barrier(piece.astype(jnp.bfloat16)).astype(
            jnp.float32
        )
    grad_weight = grad_weight.reshape(n_col * head_dim, grad_rows.shape[1])
    return (grad_weight, grad_query, grad_key, grad_value)


def solution(mesh):
    in_specs = (
        P("row", "dep", "col"),
        P("row", "col"),
        P("dep", ("row", "col")),
        P("dep", ("row", "col")),
        P("dep", ("row", "col")),
        P(),
    )
    out_specs = (
        P("row", "col"),
        P("dep", ("row", "col")),
        P("dep", ("row", "col")),
        P("dep", ("row", "col")),
    )
    return jax.shard_map(shards, mesh=mesh, in_specs=in_specs, out_specs=out_specs, check_vma=False)
```

profile of v0, /device:TPU:1, one launch (start us, length us, event | category | flops | bytes accessed | tf_op | source)
XLA Modules:
  0.0 399.3 jit_solution(16585160853598373982)
XLA Ops:
  8.1 13.7 %all_gather.18 = bf16[4,128,768]{2,1,0:T(8,128)(2,1)S(1)} all-gather(bf16[1,128,768]{2,1,0:T(8,128)(2,1)} %param.6), channel_id=1, replica_groups=mesh['row'=4,'col'=16,'dep'=4] {'row'}, dimensions={0}, use_global_device_ids=true | all-gather | bytes 983040 | tf_op jit(solution)/shard_map/all_gather | solution.py:16
  21.7 0.9 copy-done.5
  22.6 3.2 convolution_convert_fusion
  25.9 0.5 all-gather.4.cloned.1.call-update
  26.5 0.2 reduce-window.8
  26.7 0.5 copy-done.13
  27.2 0.1 convert_reduce_fusion
  27.3 0.7 convert_reduce_fusion.1
  28.0 13.8 %all_gather.15 = bf16[2048,128]{1,0:T(8,128)(2,1)S(1)} all-gather(bf16[512,128]{1,0:T(8,128)(2,1)S(1)} %copy-done.9), channel_id=1, replica_groups=mesh['row'=4,'col'=16,'dep'=4] {'dep'}, dimensions={0}, use_global_device_ids=true | all-gather | bytes 655360 | tf_op jit(solution)/shard_map/all_gather | solution.py:29
  41.9 21.1 %all_gather.16 = bf16[2048,128]{1,0:T(8,128)(2,1)} all-gather(bf16[512,128]{1,0:T(8,128)(2,1)S(1)} %copy-done.10), channel_id=1, replica_groups=mesh['row'=4,'col'=16,'dep'=4] {'dep'}, dimensions={0}, use_global_device_ids=true | all-gather | bytes 655360 | tf_op jit(solution)/shard_map/all_gather | solution.py:30
  63.0 1.3 fusion.1
  64.3 2.0 copy-done.4
  66.4 1.8 fusion.4
  68.2 64.3 %reduce-scatter.4.cloned.1.call-done = bf16[128,512]{1,0:T(8,128)(2,1)} async-done(((bf16[2048,512]{1,0:T(8,128)(2,1)}), bf16[128,512]{1,0:T(8,128)(2,1)}) %reduce-scatter.4.cloned.1.call-update) | async-done | bytes 131088 | tf_op jit(solution)/shard_map/reduce_scatter | solution.py:20
  132.4 6.5 %multiply_reduce_fusion = (f32[512]{0:T(512)S(1)}, f32[512,2048]{1,0:T(8,128)S(1)}, f32[512,2048]{1,0:T(8,128)}) fusion(f32[512]{0:T(512)S(1)} %fusion.4, f32[512]{0:T(512)S(1)} %get-tuple-element.32, f32[512,2048]{1,0:T(8,128)} %copy-done.4, s32[512]{0:T(512)S(1)} %iota_add_fusion, s32[2048]{0:T(1024)S(1)} %convert_reduce_fusion, ...), kind=kOutput, calls=%fused_computation.2 | convolution fusion | flops 278920704 | bytes 13256704 | tf_op jit(solution)/shard_map/while/body/eval_jaxpr/hq,kh->qk/dot_general | solution.py:61
  138.9 2.0 copy-done.1
  140.9 1.4 convolution_convert_fusion.6
  142.3 0.0 reduce-scatter.6.cloned.1.call-start
  142.3 3.9 multiply_convert_fusion
  146.2 1.3 copy-done.2
  147.6 1.6 fusion.2
  149.2 0.2 reduce-scatter.8.cloned.1.call-start
  149.4 3.0 fusion.5
  152.4 3.8 convolution_convert_fusion.1
  156.2 174.1 %all-gather.6.cloned.1.call-done = bf16[32768,128]{1,0:T(8,128)(2,1)} async-done(((bf16[512,128]{1,0:T(8,128)(2,1)}), bf16[32768,128]{1,0:T(8,128)(2,1)}) %all-gather.6.cloned.1.call-update) | async-done | bytes 8388624 | tf_op jit(solution)/shard_map/all_gather | solution.py:106
  330.3 3.7 convolution_convert_fusion.3
  334.1 3.9 convolution_convert_fusion.4
  338.0 1.9 convolution_convert_fusion.2
  339.8 1.9 convolution_convert_fusion.5
  341.7 4.8 %convert_add_fusion = f32[16,128,768]{2,1,0:T(8,128)} fusion(bf16[16,128,768]{2,1,0:T(8,128)(2,1)S(1)} %convolution_convert_fusion.2, bf16[16,128,768]{2,1,0:T(8,128)(2,1)S(1)} %convolution_convert_fusion.3, bf16[16,128,768]{2,1,0:T(8,128)(2,1)S(1)} %convolution_convert_fusion.4, bf16[16,128,768]{2,1,0:T(8,128)(2,1)S(1)} %convolution_convert_fusion.5), kind=kLoop, calls=%fused_computation | loop fusion | flops 11010048 | bytes 18874368 | tf_op jit(solution)/shard_map/add | solution.py:118
  346.4 16.7 %reduce-scatter.6.cloned.1.call-done = bf16[512,128]{1,0:T(8,128)(2,1)} async-done(((bf16[2048,128]{1,0:T(8,128)(2,1)}), bf16[512,128]{1,0:T(8,128)(2,1)}) %reduce-scatter.6.cloned.1.call-update) | async-done | bytes 131088 | tf_op jit(solution)/shard_map/reduce_scatter | solution.py:95
  363.2 28.5 %reduce-scatter.8.cloned.1.call-done = bf16[512,128]{1,0:T(8,128)(2,1)} async-done(((bf16[2048,128]{1,0:T(8,128)(2,1)}), bf16[512,128]{1,0:T(8,128)(2,1)}) %reduce-scatter.8.cloned.1.call-update) | async-done | bytes 131088 | tf_op jit(solution)/shard_map/reduce_scatter | solution.py:98
  (34 shorter events, 0.3 us)
Async XLA Ops:
  8.0 14.6 %copy-start = (bf16[2048,768]{1,0:T(8,128)(2,1)S(1)}, bf16[2048,768]{1,0:T(8,128)(2,1)}, u32[]{:S(2)}) copy-start(bf16[2048,768]{1,0:T(8,128)(2,1)} %param.7) | copy-start | bytes 9437188
  8.0 124.4 %reduce-scatter.4.cloned.1.call-start = ((), (), s32[]{:S(2)}) async-start(), calls=%async_computation.4 | async-start | bytes 2228224 | tf_op jit(solution)/shard_map/reduce_scatter | solution.py:20
  21.7 0.9 copy-start.5
  22.6 3.8 copy-start.14
  22.6 5.4 %copy-start.9 = (bf16[512,128]{1,0:T(8,128)(2,1)S(1)}, bf16[512,128]{1,0:T(8,128)(2,1)}, u32[]{:S(2)}) copy-start(bf16[512,128]{1,0:T(8,128)(2,1)} %param.9) | copy-start | bytes 393220
  22.6 19.2 %copy-start.10 = (bf16[512,128]{1,0:T(8,128)(2,1)S(1)}, bf16[512,128]{1,0:T(8,128)(2,1)}, u32[]{:S(2)}) copy-start(bf16[512,128]{1,0:T(8,128)(2,1)} %param.10) | copy-start | bytes 393220
  25.8 37.2 %copy-start.11 = (bf16[512,128]{1,0:T(8,128)(2,1)S(1)}, bf16[512,128]{1,0:T(8,128)(2,1)}, u32[]{:S(2)}) copy-start(bf16[512,128]{1,0:T(8,128)(2,1)} %param.8) | copy-start | bytes 393220
  25.8 130.4 %all-gather.4.cloned.1.call-start = ((), (), s32[]{:S(2)}) async-start(), calls=%async_computation.3 | async-start | bytes 3932160 | tf_op jit(solution)/shard_map/all_gather | solution.py:109
  26.4 303.9 %all-gather.6.cloned.1.call-start = ((), (), s32[]{:S(2)}) async-start(), calls=%async_computation.7 | async-start | bytes 8519680 | tf_op jit(solution)/shard_map/all_gather | solution.py:106
  26.7 0.5 copy-start.13
  41.9 21.1 %copy-start.8 = (bf16[2048,128]{1,0:T(8,128)(2,1)}, bf16[2048,128]{1,0:T(8,128)(2,1)S(1)}, u32[]{:S(2)}) copy-start(bf16[2048,128]{1,0:T(8,128)(2,1)S(1)} %all_gather.15) | copy-start | bytes 1572868
  64.3 2.0 copy-start.4
  132.4 8.4 %copy-start.7 = (bf16[2048,128]{1,0:T(8,128)(2,1)S(1)}, bf16[2048,128]{1,0:T(8,128)(2,1)}, u32[]{:S(2)}) copy-start(bf16[2048,128]{1,0:T(8,128)(2,1)} %all_gather.16) | copy-start | bytes 1572868
  138.9 2.0 copy-start.1
  142.3 220.9 %reduce-scatter.6.cloned.1.call-start = ((), (), s32[]{:S(2)}) async-start(), calls=%async_computation.5 | async-start | bytes 655360 | tf_op jit(solution)/shard_map/reduce_scatter | solution.py:95
  146.2 1.3 copy-start.2
  147.6 4.9 %copy-start.12 = (bf16[128,512]{1,0:T(8,128)(2,1)S(1)}, bf16[128,512]{1,0:T(8,128)(2,1)}, u32[]{:S(2)}) copy-start(bf16[128,512]{1,0:T(8,128)(2,1)} %reduce-scatter.4.cloned.1.call-done) | copy-start | bytes 393220
  149.2 242.5 %reduce-scatter.8.cloned.1.call-start = ((), (), s32[]{:S(2)}) async-start(), calls=%async_computation.6 | async-start | bytes 655360 | tf_op jit(solution)/shard_map/reduce_scatter | solution.py:98
  330.3 3.8 copy-start.6
  330.3 7.6 %copy-start.3 = (bf16[32768,128]{1,0:T(8,128)(2,1)S(1)}, bf16[32768,128]{1,0:T(8,128)(2,1)}, u32[]{:S(2)}) copy-start(bf16[32768,128]{1,0:T(8,128)(2,1)} %all-gather.6.cloned.1.call-done) | copy-start | bytes 25165828
Sparse Core Ops, SparseCore 0:
  26.0 106.4 reduce-scatter.3
Sparse Core Ops, SparseCore 1:
  28.1 89.4 all-gather.3
  142.4 187.9 all-gather.5
  333.3 29.8 reduce-scatter.5
  366.3 25.3 reduce-scatter.7
where the time goes:
time: 400 us; the launch traced here: 399 us
  waiting for transfers between devices  284 us (71%)
  blocking collectives  48.6 us (12%)
  matrix products  32.1 us (8%)
  between operations  15.8 us (4%)
  other arithmetic  11.5 us (3%)
  local copies, waits for them, and re-layouts  6.72 us (2%)
    all_gather x1, waiting for transfers between devices, shards(): lax.all_gather(context[None], ('col', 'dep'), axis=0, tiled=True)  174 us
    reduce_scatter x1, waiting for transfers between devices, shards(): lax.psum_scatter(jnp.einsum('hf,tf->ht', out_weight, grad_rows, preferred...  64.3 us
    reduce_scatter x1, waiting for transfers between devices, shards(): lax.psum_scatter(value_partial.astype(jnp.bfloat16), 'dep', scatter_dimen...  28.5 us
    all_gather x1, blocking collectives, shards(): lax.all_gather(value_rows, 'dep', axis=0, tiled=True)  21.1 us
    reduce_scatter x1, waiting for transfers between devices, shards(): lax.psum_scatter((key_partial * inv_root).astype(jnp.bfloat16), 'dep', sc...  16.7 us
    all_gather x1, blocking collectives, shards(): lax.all_gather(key_rows, 'dep', axis=0, tiled=True)  13.8 us
    all_gather x1, blocking collectives, shards(): lax.all_gather(grad_out, 'row', axis=0, tiled=True)  13.7 us
    dot_general x4, matrix products, shards(): jnp.einsum('cth,tf->chf', everyone[:, depth], depth_grads[depth], preferr...  11.3 us
  transfers between devices with their start and end apart: 5, of which 4 were waited for; matrix products, arithmetic and copies ran while one was open for 10% of the time, Pallas kernels for 0%

commit v1 on v0

v1 whole, which is shorter than its diff:
```python
import math

import jax
import jax.numpy as jnp
from jax import lax
from jax.sharding import Mesh
from jax.sharding import PartitionSpec as P

NEG_FILL = -1e30
COL = ("zh", "x", "core")
DEP = "zl"


def segment_count(positions, seg_ends):
    return jnp.sum((positions[:, None] >= seg_ends[None, :]).astype(jnp.int32), axis=1)


def shift(x, axis, n, s):
    return lax.ppermute(x, axis, [(i, (i + s) % n) for i in range(n)])


def pp_gather(x, axis, n):
    me = lax.axis_index(axis)
    parts = [x] + [shift(x, axis, n, -s) for s in range(1, n)]
    return jnp.roll(jnp.concatenate(parts, 0), me, axis=0)


def pp_reduce_scatter(x, axis, n):
    me = lax.axis_index(axis)
    acc = jnp.take(x, me, axis=0).astype(jnp.float32)
    for s in range(1, n):
        send = jnp.take(x, (me + s) % n, axis=0)
        acc = acc + shift(send, axis, n, s).astype(jnp.float32)
    return acc


def make_shards(n_zh, n_x, n_core, n_row, n_dep):
    def shards(grad_out, out_weight, query_rows, key_rows, value_rows, seg_lengths):
        n_tok, feat = grad_out.shape[1], grad_out.shape[2]
        tok_depth = n_row * n_tok
        head_dim = query_rows.shape[1]
        inv_root = 1.0 / math.sqrt(head_dim)

        rows_all = lax.all_gather(
            lax.all_gather(grad_out, DEP, axis=1, tiled=True), "row", axis=0, tiled=True
        ).reshape(n_row, n_dep, n_tok, feat)

        grad_rows = pp_gather(grad_out, "row", n_row).reshape(tok_depth, feat)
        partial = jnp.einsum(
            "hf,tf->ht", out_weight, grad_rows, preferred_element_type=jnp.float32
        ).astype(jnp.bfloat16)
        partial = partial.reshape(n_zh, n_x, n_core, head_dim, tok_depth)
        partial = jnp.transpose(partial, (2, 0, 1, 3, 4))
        partial = pp_reduce_scatter(partial, "core", n_core).astype(jnp.bfloat16)
        partial = jnp.transpose(partial, (1, 0, 2, 3))
        partial = pp_reduce_scatter(partial, "x", n_x).astype(jnp.bfloat16)
        context_grad = pp_reduce_scatter(partial, "zh", n_zh).astype(jnp.bfloat16).T

        kv = jnp.concatenate([key_rows, value_rows], axis=1)[None]
        kv_all = pp_gather(kv, DEP, n_dep).reshape(n_dep * tok_depth, 2 * head_dim)
        keys_all, values_all = kv_all[:, :head_dim], kv_all[:, head_dim:]
        key_total = keys_all.shape[0]
        seg_ends = jnp.cumsum(seg_lengths)
        key_pos = jnp.arange(key_total, dtype=jnp.int32)
        key_seg = segment_count(key_pos, seg_ends)
        query_pos = lax.axis_index(DEP) * tok_depth + jnp.arange(tok_depth, dtype=jnp.int32)
        query_seg = segment_count(query_pos, seg_ends)
        allowed = (query_seg[:, None] == key_seg[None, :]) & (
            key_pos[None, :] <= query_pos[:, None]
        )
        scores = (
            jnp.einsum("qh,kh->qk", query_rows, keys_all, preferred_element_type=jnp.float32)
            * inv_root
        )
        masked = jnp.where(allowed, scores, NEG_FILL)
        row_max = jnp.max(masked, axis=1, keepdims=True)
        exponent = jnp.where(allowed, jnp.exp(masked - row_max), 0.0)
        row_sum = jnp.sum(exponent, axis=1, keepdims=True)
        prob_full = exponent / row_sum
        prob_half = prob_full.astype(jnp.bfloat16)
        context = jnp.dot(prob_half, values_all, preferred_element_type=jnp.float32).astype(
            jnp.bfloat16
        )
        ctx_all = lax.all_gather(context[None], ("zh", DEP, "x", "core"), axis=0, tiled=True)
        ctx_all = ctx_all.reshape(n_zh, n_dep, n_x, n_core, tok_depth, head_dim)

        grad_prob = jnp.dot(context_grad, values_all.T, preferred_element_type=jnp.float32)
        delta_row = jnp.sum(prob_full * grad_prob, axis=1, keepdims=True)
        grad_score = (prob_full * (grad_prob - delta_row)).astype(jnp.bfloat16)
        grad_query = (
            jnp.dot(grad_score, keys_all, preferred_element_type=jnp.float32) * inv_root
        ).astype(jnp.bfloat16)
        key_partial = (
            jnp.einsum("qk,qh->kh", grad_score, query_rows, preferred_element_type=jnp.float32)
            * inv_root
        ).astype(jnp.bfloat16)
        value_partial = jnp.einsum(
            "qk,qh->kh", prob_half, context_grad, preferred_element_type=jnp.float32
        ).astype(jnp.bfloat16)
        kv_partial = jnp.concatenate([key_partial, value_partial], axis=1)
        kv_grad = pp_reduce_scatter(
            kv_partial.reshape(n_dep, tok_depth, 2 * head_dim), DEP, n_dep
        ).astype(jnp.bfloat16)
        grad_key, grad_value = kv_grad[:, :head_dim], kv_grad[:, head_dim:]

        grad_weight = jnp.zeros((n_zh, n_x, n_core, head_dim, feat), jnp.float32)
        for depth in range(n_dep):
            rows_depth = rows_all[:, depth].reshape(tok_depth, feat)
            piece = jnp.einsum(
                "zxcth,tf->zxchf",
                ctx_all[:, depth],
                rows_depth,
                preferred_element_type=jnp.float32,
            )
            grad_weight = grad_weight + lax.optimization_barrier(
                piece.astype(jnp.bfloat16)
            ).astype(jnp.float32)
        grad_weight = grad_weight.reshape(n_zh * n_x * n_core * head_dim, feat)
        return (grad_weight, grad_query, grad_key, grad_value)

    return shards


def solution(mesh):
    n_row, n_col, n_dep = mesh.shape["row"], mesh.shape["col"], mesh.shape["dep"]
    n_zh, n_core = 2, 2
    n_x = n_col // (n_zh * n_core)
    fine = Mesh(
        mesh.devices.reshape(n_row, n_zh, n_x, n_core, n_dep), ("row",) + COL + (DEP,)
    )
    in_specs = (
        P("row", DEP, COL),
        P("row", COL),
        P(DEP, ("row",) + COL),
        P(DEP, ("row",) + COL),
        P(DEP, ("row",) + COL),
        P(),
    )
    out_specs = (
        P("row", COL),
        P(DEP, ("row",) + COL),
        P(DEP, ("row",) + COL),
        P(DEP, ("row",) + COL),
    )
    return jax.shard_map(
        make_shards(n_zh, n_x, n_core, n_row, n_dep),
        mesh=fine,
        in_specs=in_specs,
        out_specs=out_specs,
        check_vma=False,
    )
```

time: 400 us -> 240 us (0.60)
  waiting for transfers between devices: 284 us -> 82.3 us
  local copies, waits for them, and re-layouts: 6.72 us -> 38.5 us
  starting transfers between devices: 0.39 us -> 30.6 us
  blocking collectives: 48.6 us -> 29.3 us
  matrix products: 32.1 us -> 22.5 us
  other arithmetic: 11.5 us -> 21.1 us
    all_gather x2, waiting for transfers between devices: 174 us -> 54.9 us  [the longest x1 54.9 us: shards(): lax.all_gather(context[None], ('zh', DEP, 'x', 'core'), axis=0, tiled=True)]
    reduce_scatter x3 -> x0, waiting for transfers between devices: 109 us -> none  [the longest x1 64.3 us: shards(): lax.psum_scatter(jnp.einsum('hf,tf->ht', out_weight, grad_rows, preferred...]
    ppermute x0 -> x14, starting transfers between devices: none -> 30.5 us  [shift(): return lax.ppermute(x, axis, [(i, (i + s) % n) for i in range(n)])]
    ppermute x0 -> x14, waiting for transfers between devices: none -> 27.4 us  [shift(): return lax.ppermute(x, axis, [(i, (i + s) % n) for i in range(n)])]
    all_gather x3 -> x1, blocking collectives: 48.6 us -> 29.3 us  [shards(): lax.all_gather(grad_out, DEP, axis=1, tiled=True)]
    unnamed x30 -> x38, local copies, waits for them, and re-layouts: 6.72 us -> 19.3 us
    reshape x0 -> x3, local copies, waits for them, and re-layouts: none -> 10.5 us  [the longest x2 9.21 us: shards(): partial = partial.reshape(n_zh, n_x, n_core, head_dim, tok_depth)]
    dot_general x10, matrix products: 28.9 us -> 19.4 us  [the longest x4 9.14 us: shards(): jnp.einsum('zxcth,tf->zxchf', ctx_all[:, depth], rows_depth, preferred_el...]
  transfers between devices with their start and end apart: 5 -> 16, of which waited for: 4 -> 7; matrix products, arithmetic and copies ran while one was open for 10% -> 28% of each run, Pallas kernels for 0% -> 0%
where the time goes in v1:
time: 240 us; the launch traced here: 239 us
  waiting for transfers between devices  82.3 us (34%)
  local copies, waits for them, and re-layouts  38.5 us (16%)
  starting transfers between devices  30.6 us (13%)
  blocking collectives  29.3 us (12%)
  matrix products  22.5 us (9%)
  other arithmetic  21.1 us (9%)
  between operations  14.5 us (6%)
    all_gather x1, waiting for transfers between devices, shards(): lax.all_gather(context[None], ('zh', DEP, 'x', 'core'), axis=0, tiled=True)  54.9 us
    ppermute x14, starting transfers between devices, shift(): return lax.ppermute(x, axis, [(i, (i + s) % n) for i in range(n)])  30.5 us
    all_gather x1, blocking collectives, shards(): lax.all_gather(grad_out, DEP, axis=1, tiled=True)  29.3 us
    ppermute x14, waiting for transfers between devices, shift(): return lax.ppermute(x, axis, [(i, (i + s) % n) for i in range(n)])  27.4 us
    unnamed x38, local copies, waits for them, and re-layouts  19.3 us
    reshape x2, local copies, waits for them, and re-layouts, shards(): partial = partial.reshape(n_zh, n_x, n_core, head_dim, tok_depth)  9.21 us
    dot_general x4, matrix products, shards(): jnp.einsum('zxcth,tf->zxchf', ctx_all[:, depth], rows_depth, preferred_el...  9.14 us
  transfers between devices with their start and end apart: 16, of which 7 were waited for; matrix products, arithmetic and copies ran while one was open for 28% of the time, Pallas kernels for 0%

profile of v1, /device:TPU:1, one launch (start us, length us, event | category | flops | bytes accessed | tf_op | source)
XLA Modules:
  0.0 238.8 jit_solution(11975935180769965620)
XLA Ops:
  7.2 3.8 %collective-permute-start.4 = (bf16[1,128,768]{2,1,0:T(8,128)(2,1)}, bf16[1,128,768]{2,1,0:T(8,128)(2,1)S(1)}, u32[]{:S(2)}, u32[]{:S(2)}) collective-permute-start(bf16[1,128,768]{2,1,0:T(8,128)(2,1)} %param.14), channel_id=1, source_target_pairs={{0,128},{64,192},{128,0},{192,64},{1,129},{65,193},{129,1},{193,65... | collective-permute-start | bytes 589832 | tf_op jit(solution)/shard_map/ppermute | solution.py:19
  12.5 1.7 maximum_bitcast_fusion
  15.9 3.0 %collective-permute-start.1 = (bf16[1,512,256]{2,1,0:T(8,128)(2,1)}, bf16[1,512,256]{2,1,0:T(8,128)(2,1)}, u32[]{:S(2)}, u32[]{:S(2)}) collective-permute-start(bf16[1,512,256]{2,1,0:T(8,128)(2,1)} %maximum_bitcast_fusion), channel_id=1, source_target_pairs={{0,2},{1,3},{2,0},{3,1},{4,6},{5,7},{6,4},{7,5},{8,10},{9,11},{10,... | collective-permute-start | bytes 786440 | tf_op jit(solution)/shard_map/ppermute | solution.py:19
  18.9 29.3 %all_gather.10 = bf16[1,512,768]{2,1,0:T(8,128)(2,1)} all-gather(bf16[1,128,768]{2,1,0:T(8,128)(2,1)} %param.14), channel_id=1, replica_groups=mesh['row'=4,'zh'=2,'x'=4,'core'=2,'zl'=4] {'zl'}, dimensions={1}, use_global_device_ids=true | all-gather | bytes 983040 | tf_op jit(solution)/shard_map/all_gather | solution.py:45
  49.8 1.7 constant_dynamic-update-slice_fusion.7
  51.8 4.1 %collective-permute-start = (bf16[1,512,256]{2,1,0:T(8,128)(2,1)}, bf16[1,512,256]{2,1,0:T(8,128)(2,1)}, u32[]{:S(2)}, u32[]{:S(2)}) collective-permute-start(bf16[1,512,256]{2,1,0:T(8,128)(2,1)} %maximum_bitcast_fusion), channel_id=1, source_target_pairs={{0,3},{1,0},{2,1},{3,2},{4,7},{5,4},{6,5},{7,6},{8,11},{9,8},{10,9... | collective-permute-start | bytes 786440 | tf_op jit(solution)/shard_map/ppermute | solution.py:19
  65.7 3.2 %fusion.2 = bf16[2048,512]{0,1:T(8,128)(2,1)} fusion(bf16[512,768]{1,0:T(8,128)(2,1)S(1)} %bitcast.140, bf16[2048,768]{1,0:T(8,128)(2,1)S(1)} %copy-done), kind=kOutput, calls=%fused_computation.9 | convolution fusion | flops 1611661312 | bytes 6029312 | tf_op jit(solution)/shard_map/hf,tf->ht/dot_general | solution.py:49
  68.8 4.4 %reshape.73 = bf16[2,4,2,128,512]{3,2,1,0,4:T(2,128)(2,1)} reshape(bf16[2048,512]{0,1:T(8,128)(2,1)} %fusion.2) | data formatting | bytes 4194304 | tf_op jit(solution)/shard_map/reshape | solution.py:52
  73.3 4.8 %copy.71 = bf16[2,4,2,128,512]{4,3,1,0,2:T(8,128)(2,1)S(1)} copy(bf16[2,4,2,128,512]{3,2,1,0,4:T(2,128)(2,1)} %reshape.73) | data formatting | bytes 4194304 | tf_op jit(solution)/shard_map/reshape | solution.py:52
  79.2 1.8 collective-permute-start.6
  81.2 1.7 constant_dynamic-update-slice_fusion.6
  82.8 1.7 constant_dynamic-update-slice_fusion.5
  84.5 1.7 constant_dynamic-update-slice_fusion.4
  93.3 1.9 fusion.7
  96.6 2.5 %collective-permute-start.8 = (bf16[2,128,512]{2,1,0:T(8,128)(2,1)S(1)}, bf16[2,128,512]{2,1,0:T(8,128)(2,1)S(1)}, u32[]{:S(2)}, u32[]{:S(2)}) collective-permute-start(bf16[2,128,512]{2,1,0:T(8,128)(2,1)S(1)} %get-tuple-element.61), channel_id=1, source_target_pairs={{0,16},{8,24},{16,0},{24,8},{1,17},{9,25},{17,1},{25,9},{2,18},{10... | collective-permute-start | bytes 786440 | tf_op jit(solution)/shard_map/ppermute | solution.py:19
  101.3 3.2 %collective-permute-done.7 = bf16[2,128,512]{2,1,0:T(8,128)(2,1)S(1)} collective-permute-done((bf16[2,128,512]{2,1,0:T(8,128)(2,1)S(1)}, bf16[2,128,512]{2,1,0:T(8,128)(2,1)S(1)}, u32[]{:S(2)}, u32[]{:S(2)}) %collective-permute-start.7) | collective-permute-done | bytes 262176 | tf_op jit(solution)/shard_map/ppermute | solution.py:19
  104.5 6.5 %collective-permute-done.8 = bf16[2,128,512]{2,1,0:T(8,128)(2,1)S(1)} collective-permute-done((bf16[2,128,512]{2,1,0:T(8,128)(2,1)S(1)}, bf16[2,128,512]{2,1,0:T(8,128)(2,1)S(1)}, u32[]{:S(2)}, u32[]{:S(2)}) %collective-permute-start.8) | collective-permute-done | bytes 262176 | tf_op jit(solution)/shard_map/ppermute | solution.py:19
  111.2 6.4 %collective-permute-start.10 = (bf16[128,512]{1,0:T(8,128)(2,1)S(1)}, bf16[128,512]{1,0:T(8,128)(2,1)S(1)}, u32[]{:S(2)}, u32[]{:S(2)}) collective-permute-start(bf16[128,512]{1,0:T(8,128)(2,1)S(1)} %select_bitcast_fusion.6), channel_id=1, source_target_pairs={{0,32},{32,0},{1,33},{33,1},{2,34},{34,2},{3,35},{35,3},{4,36},{36... | collective-permute-start | bytes 393224 | tf_op jit(solution)/shard_map/ppermute | solution.py:19
  120.8 3.6 %multiply_reduce_fusion = (f32[512]{0:T(512)S(1)}, f32[512,2048]{0,1:T(8,128)S(1)}, f32[512,2048]{0,1:T(8,128)}) fusion(f32[512]{0:T(512)S(1)} %fusion.5, f32[512]{0:T(512)S(1)} %get-tuple-element.65, f32[2048,512]{1,0:T(8,128)S(1)} %get-tuple-element.66, s32[512]{0:T(512)S(1)} %iota_add_fusion, s32[2048]{0:T(1024)S(1)} %convert_reduce_fusion, ...), kind=kOutput, calls=%fused_computation.3 | convolution fusion | flops 279248384 | bytes 13387781 | tf_op jit(solution)/shard_map/dot_general | solution.py:87
  124.4 2.0 copy-done.2
  127.9 4.7 %multiply_convert_fusion = bf16[512,2048]{0,1:T(8,128)(2,1)S(1)} fusion(f32[512,2048]{0,1:T(8,128)} %copy-done.2, f32[512,2048]{0,1:T(8,128)} %get-tuple-element.67, f32[512]{0:T(512)S(1)} %get-tuple-element.52), kind=kLoop, calls=%fused_computation.2 | loop fusion | flops 3145728 | bytes 10487808 | tf_op jit(solution)/shard_map/convert_element_type | solution.py:89
  137.0 3.3 %collective-permute-start.13 = (bf16[512,256]{1,0:T(8,128)(2,1)S(1)}, bf16[512,256]{1,0:T(8,128)(2,1)S(1)}, u32[]{:S(2)}, u32[]{:S(2)}) collective-permute-start(bf16[512,256]{1,0:T(8,128)(2,1)S(1)} %get-tuple-element.59), channel_id=1, source_target_pairs={{0,3},{1,0},{2,1},{3,2},{4,7},{5,4},{6,5},{7,6},{8,11},{9,8},{10,9... | collective-permute-start | bytes 786440 | tf_op jit(solution)/shard_map/ppermute | solution.py:19
  140.2 2.5 %fusion.6 = bf16[512,128]{1,0:T(8,128)(2,1)} fusion(bf16[512,2048]{0,1:T(8,128)(2,1)S(1)} %multiply_convert_fusion, bf16[2048,256]{1,0:T(8,128)(2,1)} %bitcast.135), kind=kOutput, calls=%fused_computation.25 | convolution fusion | flops 268566528 | bytes 2752512 | tf_op jit(solution)/shard_map/dot_general | solution.py:91
  144.1 6.9 %collective-permute-done.13 = bf16[512,256]{1,0:T(8,128)(2,1)S(1)} collective-permute-done((bf16[512,256]{1,0:T(8,128)(2,1)S(1)}, bf16[512,256]{1,0:T(8,128)(2,1)S(1)}, u32[]{:S(2)}, u32[]{:S(2)}) %collective-permute-start.13) | collective-permute-done | bytes 262176 | tf_op jit(solution)/shard_map/ppermute | solution.py:19
  151.0 7.7 %collective-permute-done.12 = bf16[512,256]{1,0:T(8,128)(2,1)S(1)} collective-permute-done((bf16[512,256]{1,0:T(8,128)(2,1)S(1)}, bf16[512,256]{1,0:T(8,128)(2,1)S(1)}, u32[]{:S(2)}, u32[]{:S(2)}) %collective-permute-start.12) | collective-permute-done | bytes 262176 | tf_op jit(solution)/shard_map/ppermute | solution.py:19
  160.5 2.1 fusion.23
  162.7 54.9 %all-gather.6.cloned.1.call-done = bf16[32768,128]{1,0:T(8,128)(2,1)} async-done(((bf16[512,128]{1,0:T(8,128)(2,1)}), bf16[32768,128]{1,0:T(8,128)(2,1)}) %all-gather.6.cloned.1.call-update) | async-done | bytes 8388624 | tf_op jit(solution)/shard_map/all_gather | solution.py:84
  217.6 3.6 %convolution_convert_fusion.3 = bf16[2,4,2,128,768]{4,3,2,1,0:T(8,128)(2,1)S(1)} fusion(bf16[512,768,1,1,1]{1,0,4,3,2:T(8,128)(2,1)S(1)} %bitcast.139, bf16[2,4,4,2,512,128]{5,4,3,2,1,0:T(8,128)(2,1)} %bitcast.143), kind=kOutput, calls=%fused_computation.14 | convolution fusion | flops 1612185600 | bytes 6029312 | tf_op jit(solution)/shard_map/zxcth,tf->zxchf/dot_general | solution.py:109
  221.6 1.9 convolution_convert_fusion.4
  223.4 1.9 convolution_convert_fusion.5
  225.3 1.9 convolution_convert_fusion.2
  227.2 4.8 %convert_add_fusion = f32[2,4,2,128,768]{4,3,2,1,0:T(8,128)} fusion(bf16[2,4,2,128,768]{4,3,2,1,0:T(8,128)(2,1)S(1)} %convolution_convert_fusion.2, bf16[2,4,2,128,768]{4,3,2,1,0:T(8,128)(2,1)S(1)} %convolution_convert_fusion.3, bf16[2,4,2,128,768]{4,3,2,1,0:T(8,128)(2,1)S(1)} %convolution_convert_fusion.4, ...), kind=kLoop, calls=%fused_computation | loop fusion | flops 11010048 | bytes 18874368 | tf_op jit(solution)/shard_map/add | solution.py:115
  (80 shorter events, 39.4 us)
Async XLA Ops:
  7.2 58.5 %copy-start = (bf16[2048,768]{1,0:T(8,128)(2,1)S(1)}, bf16[2048,768]{1,0:T(8,128)(2,1)}, u32[]{:S(2)}) copy-start(bf16[2048,768]{1,0:T(8,128)(2,1)} %param.15) | copy-start | bytes 9437188
  7.2 52.6 %copy-start.5 = (bf16[1,128,768]{2,1,0:T(8,128)(2,1)S(1)}, bf16[1,128,768]{2,1,0:T(8,128)(2,1)}, u32[]{:S(2)}) copy-start(bf16[1,128,768]{2,1,0:T(8,128)(2,1)} %param.14) | copy-start | bytes 589828
  7.2 44.3 %copy-start.12 = (s32[8]{0:T(128)S(1)}, s32[8]{0:T(128)}, u32[]{:S(2)}) copy-start(s32[8]{0:T(128)} %param.19) | copy-start | bytes 100
  7.2 153.3 %all-gather.4.cloned.1.call-start = ((), (), s32[]{:S(2)}) async-start(), calls=%async_computation | async-start | bytes 3932160 | tf_op jit(solution)/shard_map/all_gather | solution.py:44
  7.2 50.2 %collective-permute-start.4 = (bf16[1,128,768]{2,1,0:T(8,128)(2,1)}, bf16[1,128,768]{2,1,0:T(8,128)(2,1)S(1)}, u32[]{:S(2)}, u32[]{:S(2)}) collective-permute-start(bf16[1,128,768]{2,1,0:T(8,128)(2,1)} %param.14), channel_id=1, source_target_pairs={{0,128},{64,192},{128,0},{192,64},{1,129},{65,193},{129,1},{193,65... | collective-permute-start | bytes 589832 | tf_op jit(solution)/shard_map/ppermute | solution.py:19
  11.1 40.7 %collective-permute-start.3 = (bf16[1,128,768]{2,1,0:T(8,128)(2,1)}, bf16[1,128,768]{2,1,0:T(8,128)(2,1)}, u32[]{:S(2)}, u32[]{:S(2)}) collective-permute-start(bf16[1,128,768]{2,1,0:T(8,128)(2,1)} %param.14), channel_id=1, source_target_pairs={{0,192},{64,0},{128,64},{192,128},{1,193},{65,1},{129,65},{193,129... | collective-permute-start | bytes 589832 | tf_op jit(solution)/shard_map/ppermute | solution.py:19
  11.9 46.3 %collective-permute-start.5 = (bf16[1,128,768]{2,1,0:T(8,128)(2,1)}, bf16[1,128,768]{2,1,0:T(8,128)(2,1)}, u32[]{:S(2)}, u32[]{:S(2)}) collective-permute-start(bf16[1,128,768]{2,1,0:T(8,128)(2,1)} %param.14), channel_id=1, source_target_pairs={{0,64},{64,128},{128,192},{192,0},{1,65},{65,129},{129,193},{193,1... | collective-permute-start | bytes 589832 | tf_op jit(solution)/shard_map/ppermute | solution.py:19
  14.2 70.3 %collective-permute-start.2 = (bf16[1,512,256]{2,1,0:T(8,128)(2,1)}, bf16[1,512,256]{2,1,0:T(8,128)(2,1)}, u32[]{:S(2)}, u32[]{:S(2)}) collective-permute-start(bf16[1,512,256]{2,1,0:T(8,128)(2,1)} %maximum_bitcast_fusion), channel_id=1, source_target_pairs={{0,1},{1,2},{2,3},{3,0},{4,5},{5,6},{6,7},{7,4},{8,9},{9,10},{10,1... | collective-permute-start | bytes 786440 | tf_op jit(solution)/shard_map/ppermute | solution.py:19
  15.9 67.0 %collective-permute-start.1 = (bf16[1,512,256]{2,1,0:T(8,128)(2,1)}, bf16[1,512,256]{2,1,0:T(8,128)(2,1)}, u32[]{:S(2)}, u32[]{:S(2)}) collective-permute-start(bf16[1,512,256]{2,1,0:T(8,128)(2,1)} %maximum_bitcast_fusion), channel_id=1, source_target_pairs={{0,2},{1,3},{2,0},{3,1},{4,6},{5,7},{6,4},{7,5},{8,10},{9,11},{10,... | collective-permute-start | bytes 786440 | tf_op jit(solution)/shard_map/ppermute | solution.py:19
  48.2 169.4 %all-gather.6.cloned.1.call-start = ((), (), s32[]{:S(2)}) async-start(), calls=%async_computation.1 | async-start | bytes 8519680 | tf_op jit(solution)/shard_map/all_gather | solution.py:84
  51.7 17.1 %copy-start.9 = (s32[8,1]{0,1:T(1,128)}, s32[8,1]{0,1:T(1,128)S(1)}, u32[]{:S(2)}) copy-start(s32[8,1]{0,1:T(1,128)S(1)} %reduce-window.8) | copy-start | bytes 100
  51.8 29.3 %collective-permute-start = (bf16[1,512,256]{2,1,0:T(8,128)(2,1)}, bf16[1,512,256]{2,1,0:T(8,128)(2,1)}, u32[]{:S(2)}, u32[]{:S(2)}) collective-permute-start(bf16[1,512,256]{2,1,0:T(8,128)(2,1)} %maximum_bitcast_fusion), channel_id=1, source_target_pairs={{0,3},{1,0},{2,1},{3,2},{4,7},{5,4},{6,5},{7,6},{8,11},{9,8},{10,9... | collective-permute-start | bytes 786440 | tf_op jit(solution)/shard_map/ppermute | solution.py:19
  73.3 7.7 %copy-start.10 = (s32[8,1]{0,1:T(1,128)S(1)}, s32[8,1]{0,1:T(1,128)}, u32[]{:S(2)}) copy-start(s32[8,1]{0,1:T(1,128)} %copy-done.9) | copy-start | bytes 100
  73.3 12.9 %copy-start.6 = (bf16[512,128]{1,0:T(8,128)(2,1)S(1)}, bf16[512,128]{1,0:T(8,128)(2,1)}, u32[]{:S(2)}) copy-start(bf16[512,128]{1,0:T(8,128)(2,1)} %param.18) | copy-start | bytes 393220
  73.3 12.9 %copy-start.7 = (bf16[512,128]{1,0:T(8,128)(2,1)S(1)}, bf16[512,128]{1,0:T(8,128)(2,1)}, u32[]{:S(2)}) copy-start(bf16[512,128]{1,0:T(8,128)(2,1)} %param.17) | copy-start | bytes 393220
  79.2 14.1 %collective-permute-start.6 = (bf16[2,4,128,512]{3,2,1,0:T(8,128)(2,1)}, bf16[2,4,128,512]{3,2,1,0:T(8,128)(2,1)}, u32[]{:S(2)}, u32[]{:S(2)}) collective-permute-start(bf16[2,4,128,512]{3,2,1,0:T(8,128)(2,1)} %select_bitcast_fusion), channel_id=1, source_target_pairs={{0,4},{4,0},{1,5},{5,1},{2,6},{6,2},{3,7},{7,3},{8,12},{12,8},{9,1... | collective-permute-start | bytes 3145736 | tf_op jit(solution)/shard_map/ppermute | solution.py:19
  91.9 8.3 %copy-start.8 = (bf16[512,128]{1,0:T(8,128)(2,1)S(1)}, bf16[512,128]{1,0:T(8,128)(2,1)}, u32[]{:S(2)}) copy-start(bf16[512,128]{1,0:T(8,128)(2,1)} %param.16) | copy-start | bytes 393220
  93.3 31.2 %copy-start.4 = (bf16[4,512,256]{2,1,0:T(8,128)(2,1)}, bf16[4,512,256]{2,1,0:T(8,128)(2,1)S(1)}, u32[]{:S(2)}) copy-start(bf16[4,512,256]{2,1,0:T(8,128)(2,1)S(1)} %constant_dynamic-slice_fusion.1) | copy-start | bytes 3145732
  95.3 9.2 %collective-permute-start.7 = (bf16[2,128,512]{2,1,0:T(8,128)(2,1)S(1)}, bf16[2,128,512]{2,1,0:T(8,128)(2,1)S(1)}, u32[]{:S(2)}, u32[]{:S(2)}) collective-permute-start(bf16[2,128,512]{2,1,0:T(8,128)(2,1)S(1)} %fusion.16), channel_id=1, source_target_pairs={{0,8},{8,16},{16,24},{24,0},{1,9},{9,17},{17,25},{25,1},{2,10},{10... | collective-permute-start | bytes 786440 | tf_op jit(solution)/shard_map/ppermute | solution.py:19
  96.6 14.5 %collective-permute-start.8 = (bf16[2,128,512]{2,1,0:T(8,128)(2,1)S(1)}, bf16[2,128,512]{2,1,0:T(8,128)(2,1)S(1)}, u32[]{:S(2)}, u32[]{:S(2)}) collective-permute-start(bf16[2,128,512]{2,1,0:T(8,128)(2,1)S(1)} %get-tuple-element.61), channel_id=1, source_target_pairs={{0,16},{8,24},{16,0},{24,8},{1,17},{9,25},{17,1},{25,9},{2,18},{10... | collective-permute-start | bytes 786440 | tf_op jit(solution)/shard_map/ppermute | solution.py:19
  99.1 11.9 %collective-permute-start.9 = (bf16[2,128,512]{2,1,0:T(8,128)(2,1)S(1)}, bf16[2,128,512]{2,1,0:T(8,128)(2,1)S(1)}, u32[]{:S(2)}, u32[]{:S(2)}) collective-permute-start(bf16[2,128,512]{2,1,0:T(8,128)(2,1)S(1)} %get-tuple-element.62), channel_id=1, source_target_pairs={{0,24},{8,0},{16,8},{24,16},{1,25},{9,1},{17,9},{25,17},{2,26},{10... | collective-permute-start | bytes 786440 | tf_op jit(solution)/shard_map/ppermute | solution.py:19
  111.2 9.6 %collective-permute-start.10 = (bf16[128,512]{1,0:T(8,128)(2,1)S(1)}, bf16[128,512]{1,0:T(8,128)(2,1)S(1)}, u32[]{:S(2)}, u32[]{:S(2)}) collective-permute-start(bf16[128,512]{1,0:T(8,128)(2,1)S(1)} %select_bitcast_fusion.6), channel_id=1, source_target_pairs={{0,32},{32,0},{1,33},{33,1},{2,34},{34,2},{3,35},{35,3},{4,36},{36... | collective-permute-start | bytes 393224 | tf_op jit(solution)/shard_map/ppermute | solution.py:19
  124.4 2.0 copy-start.2
  127.9 5.6 %copy-start.3 = (f32[512,2048]{0,1:T(8,128)S(1)}, f32[512,2048]{0,1:T(8,128)}, u32[]{:S(2)}) copy-start(f32[512,2048]{0,1:T(8,128)} %copy-done.2) | copy-start | bytes 12582916
  136.9 7.3 %collective-permute-start.11 = (bf16[512,256]{1,0:T(8,128)(2,1)S(1)}, bf16[512,256]{1,0:T(8,128)(2,1)S(1)}, u32[]{:S(2)}, u32[]{:S(2)}) collective-permute-start(bf16[512,256]{1,0:T(8,128)(2,1)S(1)} %get-tuple-element.58), channel_id=1, source_target_pairs={{0,1},{1,2},{2,3},{3,0},{4,5},{5,6},{6,7},{7,4},{8,9},{9,10},{10,1... | collective-permute-start | bytes 786440 | tf_op jit(solution)/shard_map/ppermute | solution.py:19
  137.0 14.1 %collective-permute-start.13 = (bf16[512,256]{1,0:T(8,128)(2,1)S(1)}, bf16[512,256]{1,0:T(8,128)(2,1)S(1)}, u32[]{:S(2)}, u32[]{:S(2)}) collective-permute-start(bf16[512,256]{1,0:T(8,128)(2,1)S(1)} %get-tuple-element.59), channel_id=1, source_target_pairs={{0,3},{1,0},{2,1},{3,2},{4,7},{5,4},{6,5},{7,6},{8,11},{9,8},{10,9... | collective-permute-start | bytes 786440 | tf_op jit(solution)/shard_map/ppermute | solution.py:19
  140.2 18.5 %collective-permute-start.12 = (bf16[512,256]{1,0:T(8,128)(2,1)S(1)}, bf16[512,256]{1,0:T(8,128)(2,1)S(1)}, u32[]{:S(2)}, u32[]{:S(2)}) collective-permute-start(bf16[512,256]{1,0:T(8,128)(2,1)S(1)} %get-tuple-element.60), channel_id=1, source_target_pairs={{0,2},{1,3},{2,0},{3,1},{4,6},{5,7},{6,4},{7,5},{8,10},{9,11},{10,... | collective-permute-start | bytes 786440 | tf_op jit(solution)/shard_map/ppermute | solution.py:19
  217.6 4.0 %copy-start.11 = (bf16[32768,128]{1,0:T(8,128)(2,1)S(1)}, bf16[32768,128]{1,0:T(8,128)(2,1)}, u32[]{:S(2)}) copy-start(bf16[32768,128]{1,0:T(8,128)(2,1)} %all-gather.6.cloned.1.call-done) | copy-start | bytes 25165828
  227.2 4.8 %copy-start.1 = (bf16[2048,768]{1,0:T(8,128)(2,1)S(1)}, bf16[2048,768]{1,0:T(8,128)(2,1)}, u32[]{:S(2)}) copy-start(bf16[2048,768]{1,0:T(8,128)(2,1)} %param.15) | copy-start | bytes 9437188
Sparse Core Ops, SparseCore 0:
  48.3 45.1 all-gather.3
  127.9 89.5 all-gather.5

commit v2 on v1

v2 whole, which is shorter than its diff:
```python
import math

import jax
import jax.numpy as jnp
from jax import lax
from jax.sharding import Mesh
from jax.sharding import PartitionSpec as P

NEG_FILL = -1e30
FAR = 1 << 30
COL = ("zh", "x", "core")
DEP = "zl"


def segment_count(positions, seg_ends):
    return jnp.sum((positions[:, None] >= seg_ends[None, :]).astype(jnp.int32), axis=1)


def shift(x, axis, n, s):
    return lax.ppermute(x, axis, [(i, (i + s) % n) for i in range(n)])


def shift_open(x, axis, n, s):
    return lax.ppermute(x, axis, [(i, i + s) for i in range(n) if 0 <= i + s < n])


def roll_rows(x, amount, axis):
    size = x.shape[axis]
    doubled = jnp.concatenate([x, x], axis=axis)
    return lax.dynamic_slice_in_dim(doubled, (size - amount) % size, size, axis=axis)


def rolled_gather(x, axis, n, stack_axis=0):
    parts = [x] + [shift(x, axis, n, -s) for s in range(1, n)]
    return jnp.stack(parts, axis=stack_axis)


def pp_reduce_scatter(x, axis, n, dim):
    me = lax.axis_index(axis)
    acc = lax.dynamic_index_in_dim(x, me, dim, keepdims=False).astype(jnp.float32)
    for s in range(1, n):
        send = lax.dynamic_index_in_dim(x, (me + s) % n, dim, keepdims=False)
        acc = acc + shift(send, axis, n, s).astype(jnp.float32)
    return acc


def make_shards(n_zh, n_x, n_core, n_row, n_dep):
    def shards(grad_out, out_weight, query_rows, key_rows, value_rows, seg_lengths):
        n_tok, feat = grad_out.shape[1], grad_out.shape[2]
        tok_depth = n_row * n_tok
        head_dim = query_rows.shape[1]
        inv_root = 1.0 / math.sqrt(head_dim)
        me_r = lax.axis_index("row")
        me_d = lax.axis_index(DEP)
        local = grad_out[0]

        grad_rows = rolled_gather(local, "row", n_row).reshape(tok_depth, feat)
        partial = jnp.einsum(
            "hf,tf->ht", out_weight, grad_rows, preferred_element_type=jnp.float32
        ).astype(jnp.bfloat16)
        partial = partial.reshape(n_zh, n_x, n_core, head_dim, tok_depth)
        partial = pp_reduce_scatter(partial, "core", n_core, 2).astype(jnp.bfloat16)
        partial = pp_reduce_scatter(partial, "x", n_x, 1).astype(jnp.bfloat16)
        partial = pp_reduce_scatter(partial, "zh", n_zh, 0).astype(jnp.bfloat16)
        context_grad = roll_rows(partial.T, me_r * n_tok, 0)

        kv = jnp.concatenate([key_rows, value_rows], axis=1)
        kv_all = jnp.stack(
            [kv] + [shift_open(kv, DEP, n_dep, s) for s in range(1, n_dep)], axis=0
        ).reshape(n_dep * tok_depth, 2 * head_dim)
        keys_all, values_all = kv_all[:, :head_dim], kv_all[:, head_dim:]
        src_depth = me_d - jnp.arange(n_dep, dtype=jnp.int32)
        key_pos = (
            jnp.where(src_depth >= 0, src_depth * tok_depth, FAR)[:, None]
            + jnp.arange(tok_depth, dtype=jnp.int32)[None, :]
        ).reshape(-1)
        seg_ends = jnp.cumsum(seg_lengths)
        key_seg = segment_count(key_pos, seg_ends)
        query_pos = me_d * tok_depth + jnp.arange(tok_depth, dtype=jnp.int32)
        query_seg = segment_count(query_pos, seg_ends)
        allowed = (query_seg[:, None] == key_seg[None, :]) & (
            key_pos[None, :] <= query_pos[:, None]
        )
        scores = (
            jnp.einsum("qh,kh->qk", query_rows, keys_all, preferred_element_type=jnp.float32)
            * inv_root
        )
        masked = jnp.where(allowed, scores, NEG_FILL)
        row_max = jnp.max(masked, axis=1, keepdims=True)
        exponent = jnp.where(allowed, jnp.exp(masked - row_max), 0.0)
        row_sum = jnp.sum(exponent, axis=1, keepdims=True)
        prob_full = exponent / row_sum
        prob_half = prob_full.astype(jnp.bfloat16)
        context = jnp.dot(prob_half, values_all, preferred_element_type=jnp.float32).astype(
            jnp.bfloat16
        )
        context = roll_rows(context, -me_r * n_tok, 0)
        ctx_all = lax.all_gather(context[None], COL + (DEP,), axis=0, tiled=True)
        ctx_all = ctx_all.reshape(n_zh * n_x * n_core, n_dep * tok_depth, head_dim)

        grad_prob = jnp.dot(context_grad, values_all.T, preferred_element_type=jnp.float32)
        delta_row = jnp.sum(prob_full * grad_prob, axis=1, keepdims=True)
        grad_score = (prob_full * (grad_prob - delta_row)).astype(jnp.bfloat16)
        grad_query = (
            jnp.dot(grad_score, keys_all, preferred_element_type=jnp.float32) * inv_root
        ).astype(jnp.bfloat16)
        key_partial = (
            jnp.einsum("qk,qh->kh", grad_score, query_rows, preferred_element_type=jnp.float32)
            * inv_root
        ).astype(jnp.bfloat16)
        value_partial = jnp.einsum(
            "qk,qh->kh", prob_half, context_grad, preferred_element_type=jnp.float32
        ).astype(jnp.bfloat16)
        kv_partial = jnp.concatenate([key_partial, value_partial], axis=1).reshape(
            n_dep, tok_depth, 2 * head_dim
        )
        kv_grad = kv_partial[0].astype(jnp.float32)
        for s in range(1, n_dep):
            kv_grad = kv_grad + shift_open(kv_partial[s], DEP, n_dep, -s).astype(jnp.float32)
        kv_grad = kv_grad.astype(jnp.bfloat16)
        grad_key, grad_value = kv_grad[:, :head_dim], kv_grad[:, head_dim:]

        by_depth = roll_rows(rolled_gather(local, DEP, n_dep), me_d, 0)
        rows_all = rolled_gather(by_depth, "row", n_row, stack_axis=1)
        rows_all = rows_all.reshape(n_dep * tok_depth, feat)
        grad_weight = jnp.einsum(
            "ntk,tf->nkf", ctx_all, rows_all, preferred_element_type=jnp.float32
        ).reshape(n_zh * n_x * n_core * head_dim, feat)
        return (grad_weight, grad_query, grad_key, grad_value)

    return shards


def solution(mesh):
    n_row, n_col, n_dep = mesh.shape["row"], mesh.shape["col"], mesh.shape["dep"]
    n_zh, n_core = 2, 2
    n_x = n_col // (n_zh * n_core)
    fine = Mesh(
        mesh.devices.reshape(n_row, n_zh, n_x, n_core, n_dep), ("row",) + COL + (DEP,)
    )
    in_specs = (
        P("row", DEP, COL),
        P("row", COL),
        P(DEP, ("row",) + COL),
        P(DEP, ("row",) + COL),
        P(DEP, ("row",) + COL),
        P(),
    )
    out_specs = (
        P("row", COL),
        P(DEP, ("row",) + COL),
        P(DEP, ("row",) + COL),
        P(DEP, ("row",) + COL),
    )
    return jax.shard_map(
        make_shards(n_zh, n_x, n_core, n_row, n_dep),
        mesh=fine,
        in_specs=in_specs,
        out_specs=out_specs,
        check_vma=False,
    )
```

time: 240 us -> 338 us (1.41)
  waiting for transfers between devices: 82.3 us -> 210 us
  blocking collectives: 29.3 us -> 0 us
  other arithmetic: 21.1 us -> 11.6 us
  starting transfers between devices: 30.6 us -> 39.1 us
    ppermute x14, waiting for transfers between devices: 27.4 us -> 77.9 us  [shift(): return lax.ppermute(x, axis, [(i, (i + s) % n) for i in range(n)])]
    all_gather x2 -> x1, waiting for transfers between devices: 54.9 us -> 99.8 us  [shards(): ctx_all = lax.all_gather(context[None], COL + (DEP,), axis=0, tiled=True)]
    ppermute x0 -> x6, waiting for transfers between devices: none -> 31.8 us  [shift_open(): lax.ppermute(x, axis, [(i, i + s) for i in range(n) if 0 <= i + s < n])]
    all_gather x1 -> x0, blocking collectives: 29.3 us -> none  [shards(): lax.all_gather(grad_out, DEP, axis=1, tiled=True)]
    ppermute x0 -> x6, starting transfers between devices: none -> 15.2 us  [shift_open(): lax.ppermute(x, axis, [(i, i + s) for i in range(n) if 0 <= i + s < n])]
    reshape x1, local copies, waits for them, and re-layouts: 1.31 us -> 12.4 us  [shards(): ctx_all = ctx_all.reshape(n_zh * n_x * n_core, n_dep * tok_depth, head_dim)]
    ppermute x14, starting transfers between devices: 30.5 us -> 23.8 us  [shift(): return lax.ppermute(x, axis, [(i, (i + s) % n) for i in range(n)])]
    unnamed x38 -> x45, local copies, waits for them, and re-layouts: 19.3 us -> 13 us
  transfers between devices with their start and end apart: 16 -> 21, of which waited for: 7 -> 15; matrix products, arithmetic and copies ran while one was open for 28% -> 5% of each run, Pallas kernels for 0% -> 0%
where the time goes in v2:
time: 338 us; the launch traced here: 334 us
  waiting for transfers between devices  210 us (62%)
  starting transfers between devices  39.1 us (12%)
  local copies, waits for them, and re-layouts  35.2 us (10%)
  matrix products  23.9 us (7%)
  between operations  14.4 us (4%)
  other arithmetic  11.6 us (3%)
    all_gather x1, waiting for transfers between devices, shards(): ctx_all = lax.all_gather(context[None], COL + (DEP,), axis=0, tiled=True)  99.8 us
    ppermute x14, waiting for transfers between devices, shift(): return lax.ppermute(x, axis, [(i, (i + s) % n) for i in range(n)])  77.9 us
    ppermute x6, waiting for transfers between devices, shift_open(): lax.ppermute(x, axis, [(i, i + s) for i in range(n) if 0 <= i + s < n])  31.8 us
    ppermute x14, starting transfers between devices, shift(): return lax.ppermute(x, axis, [(i, (i + s) % n) for i in range(n)])  23.8 us
    ppermute x6, starting transfers between devices, shift_open(): lax.ppermute(x, axis, [(i, i + s) for i in range(n) if 0 <= i + s < n])  15.2 us
    unnamed x45, local copies, waits for them, and re-layouts  13 us
    reshape x1, local copies, waits for them, and re-layouts, shards(): ctx_all = ctx_all.reshape(n_zh * n_x * n_core, n_dep * tok_depth, head_dim)  12.4 us
    dot_general x1, matrix products, shards(): jnp.einsum('ntk,tf->nkf', ctx_all, rows_all, preferred_element_type=jnp.f...  11.8 us
  transfers between devices with their start and end apart: 21, of which 15 were waited for; matrix products, arithmetic and copies ran while one was open for 5% of the time, Pallas kernels for 0%

profile of v2, /device:TPU:1, one launch (start us, length us, event | category | flops | bytes accessed | tf_op | source)
XLA Modules:
  0.0 333.8 jit_solution(12385850366455091268)
XLA Ops:
  7.2 3.6 %collective-permute-start.9 = (bf16[128,768]{1,0:T(8,128)(2,1)}, bf16[128,768]{1,0:T(8,128)(2,1)S(1)}, u32[]{:S(2)}, u32[]{:S(2)}) collective-permute-start(bf16[128,768]{1,0:T(8,128)(2,1)} %bitcast.88), channel_id=1, source_target_pairs={{0,192},{64,0},{128,64},{192,128},{1,193},{65,1},{129,65},{193,129... | collective-permute-start | bytes 589832 | tf_op jit(solution)/shard_map/ppermute | solution.py:20
  11.9 7.2 %collective-permute-done.9 = bf16[128,768]{1,0:T(8,128)(2,1)S(1)} collective-permute-done((bf16[128,768]{1,0:T(8,128)(2,1)}, bf16[128,768]{1,0:T(8,128)(2,1)S(1)}, u32[]{:S(2)}, u32[]{:S(2)}) %collective-permute-start.9) | collective-permute-done | bytes 196640 | tf_op jit(solution)/shard_map/ppermute | solution.py:20
  19.1 4.6 %collective-permute-done.11 = bf16[128,768]{1,0:T(8,128)(2,1)} collective-permute-done((bf16[128,768]{1,0:T(8,128)(2,1)}, bf16[128,768]{1,0:T(8,128)(2,1)}, u32[]{:S(2)}, u32[]{:S(2)}) %collective-permute-start.11) | collective-permute-done | bytes 196640 | tf_op jit(solution)/shard_map/ppermute | solution.py:20
  24.9 3.1 fusion.1
  28.0 3.2 reshape.113
  31.2 6.3 %constant_dynamic-slice_fusion.1 = (bf16[2,4,1,128,512]{3,2,1,0,4:T(2,128)(2,1)}, bf16[2,4,1,128,512]{3,2,1,0,4:T(2,128)(2,1)}) fusion(bf16[2,4,2,128,512]{3,2,1,0,4:T(2,128)(2,1)S(1)} %reshape.113, s32[]{:T(128)S(6)} %select_n.93, s32[]{:T(128)S(6)} %select_n.95), kind=kLoop, calls=%fused_computation.71 | loop fusion | bytes 4194312 | tf_op jit(solution)/shard_map/jit(dynamic_index_in_dim)/dynamic_slice | solution.py:40
  37.6 6.0 %copy.34 = bf16[2,4,1,128,512]{4,3,1,0,2:T(8,128)(2,1)} copy(bf16[2,4,1,128,512]{3,2,1,0,4:T(2,128)(2,1)} %get-tuple-element.19) | data formatting | bytes 2097152
  44.1 4.3 %collective-permute-start = (bf16[512,256]{1,0:T(8,128)(2,1)S(1)}, bf16[512,256]{1,0:T(8,128)(2,1)}, u32[]{:S(2)}, u32[]{:S(2)}) collective-permute-start(bf16[512,256]{1,0:T(8,128)(2,1)S(1)} %constant_dynamic-update-slice_fusion), channel_id=1, source_target_pairs={{0,1},{1,2},{2,3},{4,5},{5,6},{6,7},{8,9},{9,10},{10,11},{12,13},{... | collective-permute-start | bytes 786440 | tf_op jit(solution)/shard_map/ppermute | solution.py:24
  48.4 4.9 %collective-permute-start.1 = (bf16[512,256]{1,0:T(8,128)(2,1)S(1)}, bf16[512,256]{1,0:T(8,128)(2,1)}, u32[]{:S(2)}, u32[]{:S(2)}) collective-permute-start(bf16[512,256]{1,0:T(8,128)(2,1)S(1)} %constant_dynamic-update-slice_fusion), channel_id=1, source_target_pairs={{0,2},{1,3},{4,6},{5,7},{8,10},{9,11},{12,14},{13,15},{16,18},{17,... | collective-permute-start | bytes 786440 | tf_op jit(solution)/shard_map/ppermute | solution.py:24
  53.3 2.0 collective-permute-start.2
  56.4 2.6 copy.33
  59.0 5.6 %collective-permute-done.2 = bf16[512,256]{1,0:T(8,128)(2,1)} collective-permute-done((bf16[512,256]{1,0:T(8,128)(2,1)S(1)}, bf16[512,256]{1,0:T(8,128)(2,1)}, u32[]{:S(2)}, u32[]{:S(2)}) %collective-permute-start.2) | collective-permute-done | bytes 262176 | tf_op jit(solution)/shard_map/ppermute | solution.py:24
  66.0 1.9 fusion.5
  69.2 2.5 collective-permute-start.14
  73.9 2.4 collective-permute-done.13
  76.3 6.6 %collective-permute-done.14 = bf16[2,128,512]{2,1,0:T(8,128)(2,1)S(1)} collective-permute-done((bf16[2,128,512]{2,1,0:T(8,128)(2,1)S(1)}, bf16[2,128,512]{2,1,0:T(8,128)(2,1)S(1)}, u32[]{:S(2)}, u32[]{:S(2)}) %collective-permute-start.14) | collective-permute-done | bytes 262176 | tf_op jit(solution)/shard_map/ppermute | solution.py:20
  83.1 6.1 %collective-permute-start.16 = (bf16[128,512]{1,0:T(8,128)(2,1)S(1)}, bf16[128,512]{1,0:T(8,128)(2,1)S(1)}, u32[]{:S(2)}, u32[]{:S(2)}) collective-permute-start(bf16[128,512]{1,0:T(8,128)(2,1)S(1)} %dynamic-slice_bitcast_fusion.3), channel_id=1, source_target_pairs={{0,32},{32,0},{1,33},{33,1},{2,34},{34,2},{3,35},{35,3},{4,36},{36... | collective-permute-start | bytes 393224 | tf_op jit(solution)/shard_map/ppermute | solution.py:20
  89.2 1.7 fusion.4
  90.9 4.6 %collective-permute-done.16 = bf16[128,512]{1,0:T(8,128)(2,1)S(1)} collective-permute-done((bf16[128,512]{1,0:T(8,128)(2,1)S(1)}, bf16[128,512]{1,0:T(8,128)(2,1)S(1)}, u32[]{:S(2)}, u32[]{:S(2)}) %collective-permute-start.16) | collective-permute-done | bytes 131104 | tf_op jit(solution)/shard_map/ppermute | solution.py:20
  95.5 4.0 %multiply_reduce_fusion = (f32[512]{0:T(512)S(1)}, f32[512,2048]{0,1:T(8,128)S(1)}, f32[512,2048]{0,1:T(8,128)}) fusion(f32[512]{0:T(512)S(1)} %fusion.4, f32[512]{0:T(512)S(1)} %get-tuple-element.28, f32[2048,512]{1,0:T(8,128)S(1)} %get-tuple-element.29, s32[512]{0:T(512)S(1)} %copy-done.13, s32[2048]{0:T(1024)S(1)} %bitcast.104, ...), kind=kOutput, calls=%fused_computation.2 | convolution fusion | flops 279182848 | bytes 13264900 | tf_op jit(solution)/shard_map/dot_general | solution.py:101
  102.7 5.7 %collective-permute-start.3 = (bf16[128,768]{1,0:T(8,128)(2,1)S(1)}, bf16[128,768]{1,0:T(8,128)(2,1)S(1)}, u32[]{:S(2)}, u32[]{:S(2)}) collective-permute-start(bf16[128,768]{1,0:T(8,128)(2,1)S(1)} %bitcast.91), channel_id=1, source_target_pairs={{0,3},{1,0},{2,1},{3,2},{4,7},{5,4},{6,5},{7,6},{8,11},{9,8},{10,9... | collective-permute-start | bytes 589832 | tf_op jit(solution)/shard_map/ppermute | solution.py:20
  108.8 2.3 collective-permute-done.3
  111.1 13.9 %collective-permute-done.4 = bf16[128,768]{1,0:T(8,128)(2,1)S(1)} collective-permute-done((bf16[128,768]{1,0:T(8,128)(2,1)S(1)}, bf16[128,768]{1,0:T(8,128)(2,1)S(1)}, u32[]{:S(2)}, u32[]{:S(2)}) %collective-permute-start.4) | collective-permute-done | bytes 196640 | tf_op jit(solution)/shard_map/ppermute | solution.py:20
  126.8 14.0 %collective-permute-done.6 = bf16[4,128,768]{2,1,0:T(8,128)(2,1)S(1)} collective-permute-done((bf16[4,128,768]{2,1,0:T(8,128)(2,1)S(1)}, bf16[4,128,768]{2,1,0:T(8,128)(2,1)S(1)}, u32[]{:S(2)}, u32[]{:S(2)}) %collective-permute-start.6) | collective-permute-done | bytes 786464 | tf_op jit(solution)/shard_map/ppermute | solution.py:20
  142.2 21.1 %collective-permute-done.8 = bf16[4,128,768]{2,1,0:T(8,128)(2,1)S(1)} collective-permute-done((bf16[4,128,768]{2,1,0:T(8,128)(2,1)S(1)}, bf16[4,128,768]{2,1,0:T(8,128)(2,1)S(1)}, u32[]{:S(2)}, u32[]{:S(2)}) %collective-permute-start.8) | collective-permute-done | bytes 786464 | tf_op jit(solution)/shard_map/ppermute | solution.py:20
  163.2 1.8 pad_maximum_fusion
  172.2 1.5 collective-permute-start.19
  175.1 5.8 %collective-permute-done.17 = bf16[512,256]{0,1:T(8,128)(2,1)S(1)} collective-permute-done((bf16[512,256]{0,1:T(8,128)(2,1)S(1)}, bf16[512,256]{0,1:T(8,128)(2,1)S(1)}, u32[]{:S(2)}, u32[]{:S(2)}) %collective-permute-start.17) | collective-permute-done | bytes 262176 | tf_op jit(solution)/shard_map/ppermute | solution.py:24
  180.9 20.3 %collective-permute-done.18 = bf16[512,256]{0,1:T(8,128)(2,1)S(1)} collective-permute-done((bf16[512,256]{0,1:T(8,128)(2,1)S(1)}, bf16[512,256]{0,1:T(8,128)(2,1)S(1)}, u32[]{:S(2)}, u32[]{:S(2)}) %collective-permute-start.18) | collective-permute-done | bytes 262176 | tf_op jit(solution)/shard_map/ppermute | solution.py:24
  202.9 99.8 %all-gather.3.cloned.1.call-done = bf16[32768,128]{1,0:T(8,128)(2,1)} async-done(((bf16[512,128]{1,0:T(8,128)(2,1)}), bf16[32768,128]{1,0:T(8,128)(2,1)}) %all-gather.3.cloned.1.call-update) | async-done | bytes 8388624 | tf_op jit(solution)/shard_map/all_gather | solution.py:98
  302.8 12.4 %copy.23 = bf16[16,2048,128]{1,2,0:T(8,128)(2,1)} copy(bf16[16,2048,128]{2,1,0:T(8,128)(2,1)} %bitcast.81) | data formatting | bytes 16777216 | tf_op jit(solution)/shard_map/reshape | solution.py:99
  315.1 11.8 %fusion.29 = f32[2048,768]{1,0:T(8,128)} fusion(bf16[2048,2048]{1,0:T(8,128)(2,1)} %bitcast.82, bf16[2048,768]{1,0:T(8,128)(2,1)} %bitcast.83), kind=kOutput, calls=%fused_computation.76 | convolution fusion | flops 6442450944 | bytes 17825792 | tf_op jit(solution)/shard_map/ntk,tf->nkf/dot_general | solution.py:126
  (91 shorter events, 25.7 us)
Async XLA Ops:
  7.2 17.7 %copy-start = (bf16[2048,768]{1,0:T(8,128)(2,1)S(1)}, bf16[2048,768]{1,0:T(8,128)(2,1)}, u32[]{:S(2)}) copy-start(bf16[2048,768]{1,0:T(8,128)(2,1)} %param.7) | copy-start | bytes 9437188
  7.2 295.6 %all-gather.3.cloned.1.call-start = ((), (), s32[]{:S(2)}) async-start(), calls=%async_computation | async-start | bytes 8519680 | tf_op jit(solution)/shard_map/all_gather | solution.py:98
  7.2 11.9 %collective-permute-start.9 = (bf16[128,768]{1,0:T(8,128)(2,1)}, bf16[128,768]{1,0:T(8,128)(2,1)S(1)}, u32[]{:S(2)}, u32[]{:S(2)}) collective-permute-start(bf16[128,768]{1,0:T(8,128)(2,1)} %bitcast.88), channel_id=1, source_target_pairs={{0,192},{64,0},{128,64},{192,128},{1,193},{65,1},{129,65},{193,129... | collective-permute-start | bytes 589832 | tf_op jit(solution)/shard_map/ppermute | solution.py:20
  10.9 8.2 %collective-permute-start.10 = (bf16[128,768]{1,0:T(8,128)(2,1)}, bf16[128,768]{1,0:T(8,128)(2,1)S(1)}, u32[]{:S(2)}, u32[]{:S(2)}) collective-permute-start(bf16[128,768]{1,0:T(8,128)(2,1)} %bitcast.89), channel_id=1, source_target_pairs={{0,128},{64,192},{128,0},{192,64},{1,129},{65,193},{129,1},{193,65... | collective-permute-start | bytes 589832 | tf_op jit(solution)/shard_map/ppermute | solution.py:20
  11.2 12.5 %collective-permute-start.11 = (bf16[128,768]{1,0:T(8,128)(2,1)}, bf16[128,768]{1,0:T(8,128)(2,1)}, u32[]{:S(2)}, u32[]{:S(2)}) collective-permute-start(bf16[128,768]{1,0:T(8,128)(2,1)} %bitcast.90), channel_id=1, source_target_pairs={{0,64},{64,128},{128,192},{192,0},{1,65},{65,129},{129,193},{193,1... | collective-permute-start | bytes 589832 | tf_op jit(solution)/shard_map/ppermute | solution.py:20
  37.6 6.5 %copy-start.10 = (bf16[512,128]{1,0:T(8,128)(2,1)S(1)}, bf16[512,128]{1,0:T(8,128)(2,1)}, u32[]{:S(2)}) copy-start(bf16[512,128]{1,0:T(8,128)(2,1)} %param.10) | copy-start | bytes 393220
  37.6 17.8 %copy-start.15 = (s32[8]{0:T(128)S(1)}, s32[8]{0:T(128)}, u32[]{:S(2)}) copy-start(s32[8]{0:T(128)} %param.11) | copy-start | bytes 100
  37.6 18.8 %copy-start.4 = (bf16[2,4,1,128,512]{3,2,1,0,4:T(2,128)(2,1)S(1)}, bf16[2,4,1,128,512]{3,2,1,0,4:T(2,128)(2,1)}, u32[]{:S(2)}) copy-start(bf16[2,4,1,128,512]{3,2,1,0,4:T(2,128)(2,1)} %get-tuple-element.18) | copy-start | bytes 3145732
  43.5 22.4 %collective-permute-start.12 = (bf16[2,4,128,512]{3,2,1,0:T(8,128)(2,1)}, bf16[2,4,128,512]{3,2,1,0:T(8,128)(2,1)}, u32[]{:S(2)}, u32[]{:S(2)}) collective-permute-start(bf16[2,4,128,512]{3,2,1,0:T(8,128)(2,1)} %bitcast.28), channel_id=1, source_target_pairs={{0,4},{4,0},{1,5},{5,1},{2,6},{6,2},{3,7},{7,3},{8,12},{12,8},{9,1... | collective-permute-start | bytes 3145736 | tf_op jit(solution)/shard_map/ppermute | solution.py:20
  44.1 14.9 %collective-permute-start = (bf16[512,256]{1,0:T(8,128)(2,1)S(1)}, bf16[512,256]{1,0:T(8,128)(2,1)}, u32[]{:S(2)}, u32[]{:S(2)}) collective-permute-start(bf16[512,256]{1,0:T(8,128)(2,1)S(1)} %constant_dynamic-update-slice_fusion), channel_id=1, source_target_pairs={{0,1},{1,2},{2,3},{4,5},{5,6},{6,7},{8,9},{9,10},{10,11},{12,13},{... | collective-permute-start | bytes 786440 | tf_op jit(solution)/shard_map/ppermute | solution.py:24
  48.4 10.7 %collective-permute-start.1 = (bf16[512,256]{1,0:T(8,128)(2,1)S(1)}, bf16[512,256]{1,0:T(8,128)(2,1)}, u32[]{:S(2)}, u32[]{:S(2)}) collective-permute-start(bf16[512,256]{1,0:T(8,128)(2,1)S(1)} %constant_dynamic-update-slice_fusion), channel_id=1, source_target_pairs={{0,2},{1,3},{4,6},{5,7},{8,10},{9,11},{12,14},{13,15},{16,18},{17,... | collective-permute-start | bytes 786440 | tf_op jit(solution)/shard_map/ppermute | solution.py:24
  53.3 11.4 %collective-permute-start.2 = (bf16[512,256]{1,0:T(8,128)(2,1)S(1)}, bf16[512,256]{1,0:T(8,128)(2,1)}, u32[]{:S(2)}, u32[]{:S(2)}) collective-permute-start(bf16[512,256]{1,0:T(8,128)(2,1)S(1)} %constant_dynamic-update-slice_fusion), channel_id=1, source_target_pairs={{0,3},{4,7},{8,11},{12,15},{16,19},{20,23},{24,27},{28,31},{32,35}... | collective-permute-start | bytes 786440 | tf_op jit(solution)/shard_map/ppermute | solution.py:24
  55.4 9.3 %copy-start.12 = (s32[512]{0:T(512)}, s32[512]{0:T(512)S(1)}, u32[]{:S(2)}) copy-start(s32[512]{0:T(512)S(1)} %iota_add_fusion) | copy-start | bytes 6148
  64.7 8.2 %copy-start.11 = (bf16[512,128]{1,0:T(8,128)(2,1)S(1)}, bf16[512,128]{1,0:T(8,128)(2,1)}, u32[]{:S(2)}) copy-start(bf16[512,128]{1,0:T(8,128)(2,1)} %param.8) | copy-start | bytes 393220
  64.7 8.2 %copy-start.13 = (s32[512]{0:T(512)S(1)}, s32[512]{0:T(512)}, u32[]{:S(2)}) copy-start(s32[512]{0:T(512)} %copy-done.12) | copy-start | bytes 6148
  64.7 8.2 %copy-start.14 = (s32[512]{0:T(512)S(1)}, s32[512]{0:T(512)}, u32[]{:S(2)}) copy-start(s32[512]{0:T(512)} %convert_reduce_fusion.1) | copy-start | bytes 6148
  66.0 33.6 %copy-start.6 = (bf16[4,512,256]{2,1,0:T(8,128)(2,1)}, bf16[4,512,256]{2,1,0:T(8,128)(2,1)S(1)}, u32[]{:S(2)}) copy-start(bf16[4,512,256]{2,1,0:T(8,128)(2,1)S(1)} %pad_maximum_fusion.1) | copy-start | bytes 3145732
  68.0 8.3 %collective-permute-start.13 = (bf16[2,128,512]{2,1,0:T(8,128)(2,1)S(1)}, bf16[2,128,512]{2,1,0:T(8,128)(2,1)S(1)}, u32[]{:S(2)}, u32[]{:S(2)}) collective-permute-start(bf16[2,128,512]{2,1,0:T(8,128)(2,1)S(1)} %get-tuple-element.23), channel_id=1, source_target_pairs={{0,8},{8,16},{16,24},{24,0},{1,9},{9,17},{17,25},{25,1},{2,10},{10... | collective-permute-start | bytes 786440 | tf_op jit(solution)/shard_map/ppermute | solution.py:20
  69.2 13.6 %collective-permute-start.14 = (bf16[2,128,512]{2,1,0:T(8,128)(2,1)S(1)}, bf16[2,128,512]{2,1,0:T(8,128)(2,1)S(1)}, u32[]{:S(2)}, u32[]{:S(2)}) collective-permute-start(bf16[2,128,512]{2,1,0:T(8,128)(2,1)S(1)} %get-tuple-element.25), channel_id=1, source_target_pairs={{0,16},{8,24},{16,0},{24,8},{1,17},{9,25},{17,1},{25,9},{2,18},{10... | collective-permute-start | bytes 786440 | tf_op jit(solution)/shard_map/ppermute | solution.py:20
  71.7 11.2 %collective-permute-start.15 = (bf16[2,128,512]{2,1,0:T(8,128)(2,1)S(1)}, bf16[2,128,512]{2,1,0:T(8,128)(2,1)S(1)}, u32[]{:S(2)}, u32[]{:S(2)}) collective-permute-start(bf16[2,128,512]{2,1,0:T(8,128)(2,1)S(1)} %get-tuple-element.24), channel_id=1, source_target_pairs={{0,24},{8,0},{16,8},{24,16},{1,25},{9,1},{17,9},{25,17},{2,26},{10... | collective-permute-start | bytes 786440 | tf_op jit(solution)/shard_map/ppermute | solution.py:20
  83.1 12.4 %collective-permute-start.16 = (bf16[128,512]{1,0:T(8,128)(2,1)S(1)}, bf16[128,512]{1,0:T(8,128)(2,1)S(1)}, u32[]{:S(2)}, u32[]{:S(2)}) collective-permute-start(bf16[128,512]{1,0:T(8,128)(2,1)S(1)} %dynamic-slice_bitcast_fusion.3), channel_id=1, source_target_pairs={{0,32},{32,0},{1,33},{33,1},{2,34},{34,2},{3,35},{35,3},{4,36},{36... | collective-permute-start | bytes 393224 | tf_op jit(solution)/shard_map/ppermute | solution.py:20
  102.7 8.4 %collective-permute-start.3 = (bf16[128,768]{1,0:T(8,128)(2,1)S(1)}, bf16[128,768]{1,0:T(8,128)(2,1)S(1)}, u32[]{:S(2)}, u32[]{:S(2)}) collective-permute-start(bf16[128,768]{1,0:T(8,128)(2,1)S(1)} %bitcast.91), channel_id=1, source_target_pairs={{0,3},{1,0},{2,1},{3,2},{4,7},{5,4},{6,5},{7,6},{8,11},{9,8},{10,9... | collective-permute-start | bytes 589832 | tf_op jit(solution)/shard_map/ppermute | solution.py:20
  108.4 16.6 %collective-permute-start.4 = (bf16[128,768]{1,0:T(8,128)(2,1)S(1)}, bf16[128,768]{1,0:T(8,128)(2,1)S(1)}, u32[]{:S(2)}, u32[]{:S(2)}) collective-permute-start(bf16[128,768]{1,0:T(8,128)(2,1)S(1)} %bitcast.92), channel_id=1, source_target_pairs={{0,2},{1,3},{2,0},{3,1},{4,6},{5,7},{6,4},{7,5},{8,10},{9,11},{10,... | collective-permute-start | bytes 589832 | tf_op jit(solution)/shard_map/ppermute | solution.py:20
  108.4 16.6 %collective-permute-start.5 = (bf16[128,768]{1,0:T(8,128)(2,1)S(1)}, bf16[128,768]{1,0:T(8,128)(2,1)S(1)}, u32[]{:S(2)}, u32[]{:S(2)}) collective-permute-start(bf16[128,768]{1,0:T(8,128)(2,1)S(1)} %bitcast.93), channel_id=1, source_target_pairs={{0,1},{1,2},{2,3},{3,0},{4,5},{5,6},{6,7},{7,4},{8,9},{9,10},{10,1... | collective-permute-start | bytes 589832 | tf_op jit(solution)/shard_map/ppermute | solution.py:20
  125.2 39.9 %copy-start.5 = (f32[512,2048]{0,1:T(8,128)S(1)}, f32[512,2048]{0,1:T(8,128)}, u32[]{:S(2)}) copy-start(f32[512,2048]{0,1:T(8,128)} %get-tuple-element.30) | copy-start | bytes 12582916
  125.2 15.6 %collective-permute-start.6 = (bf16[4,128,768]{2,1,0:T(8,128)(2,1)S(1)}, bf16[4,128,768]{2,1,0:T(8,128)(2,1)S(1)}, u32[]{:S(2)}, u32[]{:S(2)}) collective-permute-start(bf16[4,128,768]{2,1,0:T(8,128)(2,1)S(1)} %constant_dynamic-slice_fusion.2), channel_id=1, source_target_pairs={{0,192},{64,0},{128,64},{192,128},{1,193},{65,1},{129,65},{193,129... | collective-permute-start | bytes 2359304 | tf_op jit(solution)/shard_map/ppermute | solution.py:20
  125.3 16.9 %collective-permute-start.7 = (bf16[4,128,768]{2,1,0:T(8,128)(2,1)S(1)}, bf16[4,128,768]{2,1,0:T(8,128)(2,1)S(1)}, u32[]{:S(2)}, u32[]{:S(2)}) collective-permute-start(bf16[4,128,768]{2,1,0:T(8,128)(2,1)S(1)} %constant_dynamic-slice_fusion.2), channel_id=1, source_target_pairs={{0,128},{64,192},{128,0},{192,64},{1,129},{65,193},{129,1},{193,65... | collective-permute-start | bytes 2359304 | tf_op jit(solution)/shard_map/ppermute | solution.py:20
  125.4 37.8 %collective-permute-start.8 = (bf16[4,128,768]{2,1,0:T(8,128)(2,1)S(1)}, bf16[4,128,768]{2,1,0:T(8,128)(2,1)S(1)}, u32[]{:S(2)}, u32[]{:S(2)}) collective-permute-start(bf16[4,128,768]{2,1,0:T(8,128)(2,1)S(1)} %constant_dynamic-slice_fusion.2), channel_id=1, source_target_pairs={{0,64},{64,128},{128,192},{192,0},{1,65},{65,129},{129,193},{193,1... | collective-permute-start | bytes 2359304 | tf_op jit(solution)/shard_map/ppermute | solution.py:20
  169.6 11.3 %collective-permute-start.17 = (bf16[512,256]{0,1:T(8,128)(2,1)S(1)}, bf16[512,256]{0,1:T(8,128)(2,1)S(1)}, u32[]{:S(2)}, u32[]{:S(2)}) collective-permute-start(bf16[512,256]{0,1:T(8,128)(2,1)S(1)} %get-tuple-element.20), channel_id=1, source_target_pairs={{1,0},{2,1},{3,2},{5,4},{6,5},{7,6},{9,8},{10,9},{11,10},{13,12},{... | collective-permute-start | bytes 786440 | tf_op jit(solution)/shard_map/ppermute | solution.py:24
  170.9 30.3 %collective-permute-start.18 = (bf16[512,256]{0,1:T(8,128)(2,1)S(1)}, bf16[512,256]{0,1:T(8,128)(2,1)S(1)}, u32[]{:S(2)}, u32[]{:S(2)}) collective-permute-start(bf16[512,256]{0,1:T(8,128)(2,1)S(1)} %get-tuple-element.22), channel_id=1, source_target_pairs={{2,0},{3,1},{6,4},{7,5},{10,8},{11,9},{14,12},{15,13},{18,16},{19,... | collective-permute-start | bytes 786440 | tf_op jit(solution)/shard_map/ppermute | solution.py:24
  172.2 29.0 %collective-permute-start.19 = (bf16[512,256]{0,1:T(8,128)(2,1)S(1)}, bf16[512,256]{0,1:T(8,128)(2,1)S(1)}, u32[]{:S(2)}, u32[]{:S(2)}) collective-permute-start(bf16[512,256]{0,1:T(8,128)(2,1)S(1)} %get-tuple-element.21), channel_id=1, source_target_pairs={{3,0},{7,4},{11,8},{15,12},{19,16},{23,20},{27,24},{31,28},{35,32}... | collective-permute-start | bytes 786440 | tf_op jit(solution)/shard_map/ppermute | solution.py:24
  315.1 11.8 %copy-start.1 = (bf16[2048,768]{1,0:T(8,128)(2,1)S(1)}, bf16[2048,768]{1,0:T(8,128)(2,1)}, u32[]{:S(2)}) copy-start(bf16[2048,768]{1,0:T(8,128)(2,1)} %param.7) | copy-start | bytes 9437188
  (5 other events, 20.0 us)
Sparse Core Ops, SparseCore 0:
  102.8 199.9 all-gather.2

commit v3 on v2

--- a/solution.py
+++ b/solution.py
@@ -56,13 +56,13 @@
 
         grad_rows = rolled_gather(local, "row", n_row).reshape(tok_depth, feat)
         partial = jnp.einsum(
-            "hf,tf->ht", out_weight, grad_rows, preferred_element_type=jnp.float32
+            "tf,hf->th", grad_rows, out_weight, preferred_element_type=jnp.float32
         ).astype(jnp.bfloat16)
-        partial = partial.reshape(n_zh, n_x, n_core, head_dim, tok_depth)
-        partial = pp_reduce_scatter(partial, "core", n_core, 2).astype(jnp.bfloat16)
-        partial = pp_reduce_scatter(partial, "x", n_x, 1).astype(jnp.bfloat16)
-        partial = pp_reduce_scatter(partial, "zh", n_zh, 0).astype(jnp.bfloat16)
-        context_grad = roll_rows(partial.T, me_r * n_tok, 0)
+        partial = partial.reshape(tok_depth, n_zh, n_x, n_core, head_dim)
+        partial = pp_reduce_scatter(partial, "core", n_core, 3).astype(jnp.bfloat16)
+        partial = pp_reduce_scatter(partial, "x", n_x, 2).astype(jnp.bfloat16)
+        partial = pp_reduce_scatter(partial, "zh", n_zh, 1).astype(jnp.bfloat16)
+        context_grad = roll_rows(partial, me_r * n_tok, 0)
 
         kv = jnp.concatenate([key_rows, value_rows], axis=1)
         kv_all = jnp.stack(
@@ -94,9 +94,12 @@
         context = jnp.dot(prob_half, values_all, preferred_element_type=jnp.float32).astype(
             jnp.bfloat16
         )
+        by_depth = roll_rows(rolled_gather(local, DEP, n_dep), me_d, 0)
+        rows_all = rolled_gather(by_depth, "row", n_row, stack_axis=1)
         context = roll_rows(context, -me_r * n_tok, 0)
-        ctx_all = lax.all_gather(context[None], COL + (DEP,), axis=0, tiled=True)
-        ctx_all = ctx_all.reshape(n_zh * n_x * n_core, n_dep * tok_depth, head_dim)
+        context, rows_all = lax.optimization_barrier((context, rows_all))
+        ctx_all = lax.all_gather(context[None], ("zh", DEP, "x", "core"), axis=0, tiled=True)
+        ctx_all = ctx_all.reshape(n_zh, n_dep, n_x, n_core, tok_depth, head_dim)
 
         grad_prob = jnp.dot(context_grad, values_all.T, preferred_element_type=jnp.float32)
         delta_row = jnp.sum(prob_full * grad_prob, axis=1, keepdims=True)
@@ -120,12 +123,16 @@
         kv_grad = kv_grad.astype(jnp.bfloat16)
         grad_key, grad_value = kv_grad[:, :head_dim], kv_grad[:, head_dim:]
 
-        by_depth = roll_rows(rolled_gather(local, DEP, n_dep), me_d, 0)
-        rows_all = rolled_gather(by_depth, "row", n_row, stack_axis=1)
-        rows_all = rows_all.reshape(n_dep * tok_depth, feat)
-        grad_weight = jnp.einsum(
-            "ntk,tf->nkf", ctx_all, rows_all, preferred_element_type=jnp.float32
-        ).reshape(n_zh * n_x * n_core * head_dim, feat)
+        grad_weight = None
+        for depth in range(n_dep):
+            piece = jnp.einsum(
+                "zxcth,tf->zxchf",
+                ctx_all[:, depth],
+                rows_all[depth].reshape(tok_depth, feat),
+                preferred_element_type=jnp.float32,
+            )
+            grad_weight = piece if grad_weight is None else grad_weight + piece
+        grad_weight = grad_weight.reshape(n_zh * n_x * n_core * head_dim, feat)
         return (grad_weight, grad_query, grad_key, grad_value)
 
     return shards

time: 338 us -> 214 us (0.63); the launches traced: 334 us -> 213 us
  waiting for transfers between devices: 210 us -> 94.2 us
  local copies, waits for them, and re-layouts: 35.2 us -> 23.5 us
  other arithmetic: 11.6 us -> 15.5 us
  matrix products: 23.9 us -> 27.5 us
    ppermute x14, waiting for transfers between devices: 77.9 us -> 19.8 us  [shift(): return lax.ppermute(x, axis, [(i, (i + s) % n) for i in range(n)])]
    all_gather x1, waiting for transfers between devices: 99.8 us -> 53.2 us  [shards(): lax.all_gather(context[None], ('zh', DEP, 'x', 'core'), axis=0, tiled=True)]
    reshape x2 -> x1, local copies, waits for them, and re-layouts: 15.6 us -> 3.26 us  [shards(): partial = partial.reshape(tok_depth, n_zh, n_x, n_core, head_dim)]
    ppermute x6, waiting for transfers between devices: 31.8 us -> 21.2 us  [shift_open(): lax.ppermute(x, axis, [(i, i + s) for i in range(n) if 0 <= i + s < n])]
    ppermute x6, starting transfers between devices: 15.2 us -> 10.8 us  [shift_open(): lax.ppermute(x, axis, [(i, i + s) for i in range(n) if 0 <= i + s < n])]
    ppermute x14, starting transfers between devices: 23.8 us -> 27.4 us  [shift(): return lax.ppermute(x, axis, [(i, (i + s) % n) for i in range(n)])]
    convert_element_type x1, other arithmetic: 1.16 us -> 4.74 us  [shards(): grad_score = (prob_full * (grad_prob - delta_row)).astype(jnp.bfloat16)]
    dot_general x2 -> x5, matrix products: 14.9 us -> 17 us  [the longest x4 13.8 us: shards(): jnp.einsum('zxcth,tf->zxchf', ctx_all[:, depth], rows_all[depth].reshape(...]
  transfers between devices with their start and end apart: 21 -> 21, of which waited for: 15 -> 8; matrix products, arithmetic and copies ran while one was open for 5% -> 20% of each run, Pallas kernels for 0% -> 0%
where the time goes in v3:
time: 214 us; the launch traced here: 213 us
  waiting for transfers between devices  94.2 us (44%)
  starting transfers between devices  38.3 us (18%)
  matrix products  27.5 us (13%)
  local copies, waits for them, and re-layouts  23.5 us (11%)
  other arithmetic  15.5 us (7%)
  between operations  14.4 us (7%)
    all_gather x1, waiting for transfers between devices, shards(): lax.all_gather(context[None], ('zh', DEP, 'x', 'core'), axis=0, tiled=True)  53.2 us
    ppermute x14, starting transfers between devices, shift(): return lax.ppermute(x, axis, [(i, (i + s) % n) for i in range(n)])  27.4 us
    ppermute x6, waiting for transfers between devices, shift_open(): lax.ppermute(x, axis, [(i, i + s) for i in range(n) if 0 <= i + s < n])  21.2 us
    ppermute x14, waiting for transfers between devices, shift(): return lax.ppermute(x, axis, [(i, (i + s) % n) for i in range(n)])  19.8 us
    dot_general x4, matrix products, shards(): jnp.einsum('zxcth,tf->zxchf', ctx_all[:, depth], rows_all[depth].reshape(...  13.8 us
    unnamed x46, local copies, waits for them, and re-layouts  12.4 us
    ppermute x6, starting transfers between devices, shift_open(): lax.ppermute(x, axis, [(i, i + s) for i in range(n) if 0 <= i + s < n])  10.8 us
    dot_general x1, matrix products, shards(): jnp.dot(context_grad, values_all.T, preferred_element_type=jnp.float32)  5.32 us
  transfers between devices with their start and end apart: 21, of which 8 were waited for; matrix products, arithmetic and copies ran while one was open for 20% of the time, Pallas kernels for 0%

profile of v3, /device:TPU:1, one launch (start us, length us, event | category | flops | bytes accessed | tf_op | source)
XLA Modules:
  0.0 213.4 jit_solution(14504778845396095603)
XLA Ops:
  7.2 2.2 %collective-permute-start.11 = (bf16[128,768]{1,0:T(8,128)(2,1)}, bf16[128,768]{1,0:T(8,128)(2,1)}, u32[]{:S(2)}, u32[]{:S(2)}) collective-permute-start(bf16[128,768]{1,0:T(8,128)(2,1)} %bitcast.123), channel_id=1, source_target_pairs={{0,64},{64,128},{128,192},{192,0},{1,65},{65,129},{129,193},{193,1... | collective-permute-start | bytes 589832 | tf_op jit(solution)/shard_map/ppermute | solution.py:20
  9.4 2.6 %collective-permute-start.10 = (bf16[128,768]{1,0:T(8,128)(2,1)}, bf16[128,768]{1,0:T(8,128)(2,1)}, u32[]{:S(2)}, u32[]{:S(2)}) collective-permute-start(bf16[128,768]{1,0:T(8,128)(2,1)} %bitcast.124), channel_id=1, source_target_pairs={{0,128},{64,192},{128,0},{192,64},{1,129},{65,193},{129,1},{193,65... | collective-permute-start | bytes 589832 | tf_op jit(solution)/shard_map/ppermute | solution.py:20
  13.1 1.6 collective-permute-start.5
  14.8 3.0 %collective-permute-start.4 = (bf16[128,768]{1,0:T(8,128)(2,1)}, bf16[128,768]{1,0:T(8,128)(2,1)S(1)}, u32[]{:S(2)}, u32[]{:S(2)}) collective-permute-start(bf16[128,768]{1,0:T(8,128)(2,1)} %bitcast.127), channel_id=1, source_target_pairs={{0,2},{1,3},{2,0},{3,1},{4,6},{5,7},{6,4},{7,5},{8,10},{9,11},{10,... | collective-permute-start | bytes 589832 | tf_op jit(solution)/shard_map/ppermute | solution.py:20
  22.1 1.6 constant_dynamic-update-slice_fusion
  25.0 1.6 constant_dynamic-update-slice_fusion.3
  27.4 3.1 %collective-permute-start.2 = (bf16[512,256]{1,0:T(8,128)(2,1)}, bf16[512,256]{1,0:T(8,128)(2,1)}, u32[]{:S(2)}, u32[]{:S(2)}) collective-permute-start(bf16[512,256]{1,0:T(8,128)(2,1)} %constant_dynamic-update-slice_fusion), channel_id=1, source_target_pairs={{0,3},{4,7},{8,11},{12,15},{16,19},{20,23},{24,27},{28,31},{32,35}... | collective-permute-start | bytes 786440 | tf_op jit(solution)/shard_map/ppermute | solution.py:24
  30.5 2.0 collective-permute-start.1
  33.8 3.1 %convolution_convert_fusion = bf16[512,2048]{1,0:T(8,128)(2,1)} fusion(bf16[512,768]{1,0:T(8,128)(2,1)S(1)} %bitcast.133, bf16[2048,768]{1,0:T(8,128)(2,1)S(1)} %copy-done), kind=kOutput, calls=%fused_computation.8 | convolution fusion | flops 1611661312 | bytes 6029312 | tf_op jit(solution)/shard_map/tf,hf->th/dot_general | solution.py:58
  36.9 3.3 %reshape.111 = bf16[512,2,4,2,128]{4,3,2,1,0:T(2,128)(2,1)S(1)} reshape(bf16[512,2048]{1,0:T(8,128)(2,1)} %convolution_convert_fusion) | data formatting | bytes 4194304 | tf_op jit(solution)/shard_map/reshape | solution.py:61
  41.7 1.6 bitcast_dynamic-update-slice_fusion.4
  45.4 4.3 %constant_dynamic-slice_fusion.1 = (bf16[512,2,4,1,128]{4,3,2,1,0:T(2,128)(2,1)S(1)}, bf16[512,2,4,1,128]{4,3,2,1,0:T(2,128)(2,1)S(1)}) fusion(bf16[512,2,4,2,128]{4,3,2,1,0:T(2,128)(2,1)S(1)} %reshape.111, s32[]{:T(128)S(6)} %select_n.93, s32[]{:T(128)S(6)} %select_n.95), kind=kLoop, calls=%fused_computation.79 | loop fusion | bytes 4194312 | tf_op jit(solution)/shard_map/jit(dynamic_index_in_dim)/dynamic_slice | solution.py:40
  50.1 2.9 %collective-permute-start.12 = (bf16[512,2,4,128]{3,0,2,1:T(8,128)(2,1)S(1)}, bf16[512,2,4,128]{3,0,2,1:T(8,128)(2,1)S(1)}, u32[]{:S(2)}, u32[]{:S(2)}) collective-permute-start(bf16[512,2,4,128]{3,0,2,1:T(8,128)(2,1)S(1)} %bitcast.129), channel_id=1, source_target_pairs={{0,4},{4,0},{1,5},{5,1},{2,6},{6,2},{3,7},{7,3},{8,12},{12,8},{9,1... | collective-permute-start | bytes 3145736 | tf_op jit(solution)/shard_map/ppermute | solution.py:20
  54.4 2.8 %collective-permute-start.6 = (bf16[4,128,768]{2,1,0:T(8,128)(2,1)S(1)}, bf16[4,128,768]{2,1,0:T(8,128)(2,1)S(1)}, u32[]{:S(2)}, u32[]{:S(2)}) collective-permute-start(bf16[4,128,768]{2,1,0:T(8,128)(2,1)S(1)} %constant_dynamic-slice_fusion.2), channel_id=1, source_target_pairs={{0,192},{64,0},{128,64},{192,128},{1,193},{65,1},{129,65},{193,129... | collective-permute-start | bytes 2359304 | tf_op jit(solution)/shard_map/ppermute | solution.py:20
  62.8 4.7 %collective-permute-done.13 = bf16[512,2,128]{2,0,1:T(8,128)(2,1)S(1)} collective-permute-done((bf16[512,2,128]{2,0,1:T(8,128)(2,1)S(1)}, bf16[512,2,128]{2,0,1:T(8,128)(2,1)S(1)}, u32[]{:S(2)}, u32[]{:S(2)}) %collective-permute-start.13) | collective-permute-done | bytes 262176 | tf_op jit(solution)/shard_map/ppermute | solution.py:20
  69.0 1.7 fusion.3
  70.8 4.6 %collective-permute-done.14 = bf16[512,2,128]{2,0,1:T(8,128)(2,1)S(1)} collective-permute-done((bf16[512,2,128]{2,0,1:T(8,128)(2,1)S(1)}, bf16[512,2,128]{2,0,1:T(8,128)(2,1)S(1)}, u32[]{:S(2)}, u32[]{:S(2)}) %collective-permute-start.14) | collective-permute-done | bytes 262176 | tf_op jit(solution)/shard_map/ppermute | solution.py:20
  75.5 6.0 %collective-permute-start.16 = (bf16[512,128]{1,0:T(8,128)(2,1)S(1)}, bf16[512,128]{1,0:T(8,128)(2,1)S(1)}, u32[]{:S(2)}, u32[]{:S(2)}) collective-permute-start(bf16[512,128]{1,0:T(8,128)(2,1)S(1)} %dynamic-slice_bitcast_fusion.3), channel_id=1, source_target_pairs={{0,32},{32,0},{1,33},{33,1},{2,34},{34,2},{3,35},{35,3},{4,36},{36... | collective-permute-start | bytes 393224 | tf_op jit(solution)/shard_map/ppermute | solution.py:20
  81.5 7.8 %collective-permute-done.6 = bf16[4,128,768]{2,1,0:T(8,128)(2,1)S(1)} collective-permute-done((bf16[4,128,768]{2,1,0:T(8,128)(2,1)S(1)}, bf16[4,128,768]{2,1,0:T(8,128)(2,1)S(1)}, u32[]{:S(2)}, u32[]{:S(2)}) %collective-permute-start.6) | collective-permute-done | bytes 786464 | tf_op jit(solution)/shard_map/ppermute | solution.py:20
  89.3 2.7 %collective-permute-done.8 = bf16[4,128,768]{2,1,0:T(8,128)(2,1)S(1)} collective-permute-done((bf16[4,128,768]{2,1,0:T(8,128)(2,1)S(1)}, bf16[4,128,768]{2,1,0:T(8,128)(2,1)S(1)}, u32[]{:S(2)}, u32[]{:S(2)}) %collective-permute-start.8) | collective-permute-done | bytes 786464 | tf_op jit(solution)/shard_map/ppermute | solution.py:20
  92.5 5.3 %multiply_reduce_fusion = (f32[512]{0:T(512)S(1)}, f32[512,2048]{0,1:T(8,128)S(1)}, f32[512,2048]{0,1:T(8,128)}) fusion(f32[512]{0:T(512)S(1)} %fusion.3, f32[512]{0:T(512)S(1)} %get-tuple-element.36, f32[2048,512]{1,0:T(8,128)S(1)} %get-tuple-element.37, s32[512]{0:T(512)S(1)} %copy-done.15, s32[2048]{0:T(1024)S(1)} %bitcast.139, ...), kind=kOutput, calls=%fused_computation.3 | convolution fusion | flops 279182848 | bytes 13264900 | tf_op jit(solution)/shard_map/dot_general | solution.py:104
  97.8 2.0 copy-done.2
  101.8 4.7 %multiply_convert_fusion = bf16[512,2048]{0,1:T(8,128)(2,1)S(1)} fusion(f32[512,2048]{0,1:T(8,128)} %copy-done.2, f32[512,2048]{0,1:T(8,128)} %get-tuple-element.38, f32[512]{0:T(512)S(1)} %get-tuple-element.20), kind=kLoop, calls=%fused_computation.2 | loop fusion | flops 3145728 | bytes 10487808 | tf_op jit(solution)/shard_map/convert_element_type | solution.py:106
  112.9 1.7 fusion.29
  116.0 4.9 %collective-permute-done.17 = bf16[512,256]{0,1:T(8,128)(2,1)S(1)} collective-permute-done((bf16[512,256]{0,1:T(8,128)(2,1)S(1)}, bf16[512,256]{0,1:T(8,128)(2,1)S(1)}, u32[]{:S(2)}, u32[]{:S(2)}) %collective-permute-start.17) | collective-permute-done | bytes 262176 | tf_op jit(solution)/shard_map/ppermute | solution.py:24
  121.0 3.9 %collective-permute-done.19 = bf16[512,256]{0,1:T(8,128)(2,1)S(1)} collective-permute-done((bf16[512,256]{0,1:T(8,128)(2,1)S(1)}, bf16[512,256]{0,1:T(8,128)(2,1)S(1)}, u32[]{:S(2)}, u32[]{:S(2)}) %collective-permute-start.19) | collective-permute-done | bytes 262176 | tf_op jit(solution)/shard_map/ppermute | solution.py:24
  124.9 12.4 %collective-permute-done.18 = bf16[512,256]{0,1:T(8,128)(2,1)S(1)} collective-permute-done((bf16[512,256]{0,1:T(8,128)(2,1)S(1)}, bf16[512,256]{0,1:T(8,128)(2,1)S(1)}, u32[]{:S(2)}, u32[]{:S(2)}) %collective-permute-start.18) | collective-permute-done | bytes 262176 | tf_op jit(solution)/shard_map/ppermute | solution.py:24
  139.0 53.2 %all-gather.3.cloned.1.call-done = bf16[32768,128]{1,0:T(8,128)(2,1)} async-done(((bf16[512,128]{1,0:T(8,128)(2,1)}), bf16[32768,128]{1,0:T(8,128)(2,1)}) %all-gather.3.cloned.1.call-update) | async-done | bytes 8388624 | tf_op jit(solution)/shard_map/all_gather | solution.py:101
  192.1 3.6 %fusion.4 = f32[2,4,2,128,768]{4,3,2,1,0:T(8,128)S(1)} fusion(bf16[512,768,1,1,1]{1,0,4,3,2:T(8,128)(2,1)S(1)} %bitcast.118, bf16[2,4,4,2,512,128]{5,4,3,2,1,0:T(8,128)(2,1)} %bitcast.110), kind=kOutput, calls=%fused_computation.16 | convolution fusion | flops 1610612736 | bytes 9175040 | tf_op jit(solution)/shard_map/zxcth,tf->zxchf/dot_general | solution.py:128
  196.3 1.9 fusion.5
  198.2 1.9 fusion.6
  200.1 6.5 %add_add_fusion = f32[2,4,2,128,768]{4,3,2,1,0:T(8,128)} fusion(f32[2,4,2,128,768]{4,3,2,1,0:T(8,128)S(1)} %fusion.4, f32[2,4,2,128,768]{4,3,2,1,0:T(8,128)S(1)} %fusion.6, f32[2,4,2,128,768]{4,3,2,1,0:T(8,128)S(1)} %fusion.5, bf16[512,768,1,1,1]{1,0,4,3,2:T(8,128)(2,1)S(1)} %bitcast.115, bf16[2,4,4,2,512,128]{5,4,3,2,1,0:T(8,128)(2,1)} %bitcast.111), kind=kOutput, calls=%fused_computation | convolution fusion | flops 1615331328 | bytes 28049408 | tf_op jit(solution)/shard_map/zxcth,tf->zxchf/dot_general | solution.py:128
  (95 shorter events, 33.8 us)
Async XLA Ops:
  7.2 26.6 %copy-start = (bf16[2048,768]{1,0:T(8,128)(2,1)S(1)}, bf16[2048,768]{1,0:T(8,128)(2,1)}, u32[]{:S(2)}) copy-start(bf16[2048,768]{1,0:T(8,128)(2,1)} %param.7) | copy-start | bytes 9437188
  7.2 184.9 %all-gather.3.cloned.1.call-start = ((), (), s32[]{:S(2)}) async-start(), calls=%async_computation | async-start | bytes 8519680 | tf_op jit(solution)/shard_map/all_gather | solution.py:101
  7.2 19.4 %collective-permute-start.11 = (bf16[128,768]{1,0:T(8,128)(2,1)}, bf16[128,768]{1,0:T(8,128)(2,1)}, u32[]{:S(2)}, u32[]{:S(2)}) collective-permute-start(bf16[128,768]{1,0:T(8,128)(2,1)} %bitcast.123), channel_id=1, source_target_pairs={{0,64},{64,128},{128,192},{192,0},{1,65},{65,129},{129,193},{193,1... | collective-permute-start | bytes 589832 | tf_op jit(solution)/shard_map/ppermute | solution.py:20
  9.4 17.9 %collective-permute-start.10 = (bf16[128,768]{1,0:T(8,128)(2,1)}, bf16[128,768]{1,0:T(8,128)(2,1)}, u32[]{:S(2)}, u32[]{:S(2)}) collective-permute-start(bf16[128,768]{1,0:T(8,128)(2,1)} %bitcast.124), channel_id=1, source_target_pairs={{0,128},{64,192},{128,0},{192,64},{1,129},{65,193},{129,1},{193,65... | collective-permute-start | bytes 589832 | tf_op jit(solution)/shard_map/ppermute | solution.py:20
  12.1 18.4 %collective-permute-start.9 = (bf16[128,768]{1,0:T(8,128)(2,1)}, bf16[128,768]{1,0:T(8,128)(2,1)}, u32[]{:S(2)}, u32[]{:S(2)}) collective-permute-start(bf16[128,768]{1,0:T(8,128)(2,1)} %bitcast.125), channel_id=1, source_target_pairs={{0,192},{64,0},{128,64},{192,128},{1,193},{65,1},{129,65},{193,129... | collective-permute-start | bytes 589832 | tf_op jit(solution)/shard_map/ppermute | solution.py:20
  13.1 30.9 %collective-permute-start.5 = (bf16[128,768]{1,0:T(8,128)(2,1)}, bf16[128,768]{1,0:T(8,128)(2,1)S(1)}, u32[]{:S(2)}, u32[]{:S(2)}) collective-permute-start(bf16[128,768]{1,0:T(8,128)(2,1)} %bitcast.126), channel_id=1, source_target_pairs={{0,1},{1,2},{2,3},{3,0},{4,5},{5,6},{6,7},{7,4},{8,9},{9,10},{10,1... | collective-permute-start | bytes 589832 | tf_op jit(solution)/shard_map/ppermute | solution.py:20
  14.8 28.6 %collective-permute-start.4 = (bf16[128,768]{1,0:T(8,128)(2,1)}, bf16[128,768]{1,0:T(8,128)(2,1)S(1)}, u32[]{:S(2)}, u32[]{:S(2)}) collective-permute-start(bf16[128,768]{1,0:T(8,128)(2,1)} %bitcast.127), channel_id=1, source_target_pairs={{0,2},{1,3},{2,0},{3,1},{4,6},{5,7},{6,4},{7,5},{8,10},{9,11},{10,... | collective-permute-start | bytes 589832 | tf_op jit(solution)/shard_map/ppermute | solution.py:20
  26.6 13.6 %collective-permute-start.3 = (bf16[128,768]{1,0:T(8,128)(2,1)}, bf16[128,768]{1,0:T(8,128)(2,1)}, u32[]{:S(2)}, u32[]{:S(2)}) collective-permute-start(bf16[128,768]{1,0:T(8,128)(2,1)} %bitcast.128), channel_id=1, source_target_pairs={{0,3},{1,0},{2,1},{3,2},{4,7},{5,4},{6,5},{7,6},{8,11},{9,8},{10,9... | collective-permute-start | bytes 589832 | tf_op jit(solution)/shard_map/ppermute | solution.py:20
  27.4 27.0 %collective-permute-start.2 = (bf16[512,256]{1,0:T(8,128)(2,1)}, bf16[512,256]{1,0:T(8,128)(2,1)}, u32[]{:S(2)}, u32[]{:S(2)}) collective-permute-start(bf16[512,256]{1,0:T(8,128)(2,1)} %constant_dynamic-update-slice_fusion), channel_id=1, source_target_pairs={{0,3},{4,7},{8,11},{12,15},{16,19},{20,23},{24,27},{28,31},{32,35}... | collective-permute-start | bytes 786440 | tf_op jit(solution)/shard_map/ppermute | solution.py:24
  30.5 26.7 %collective-permute-start.1 = (bf16[512,256]{1,0:T(8,128)(2,1)}, bf16[512,256]{1,0:T(8,128)(2,1)}, u32[]{:S(2)}, u32[]{:S(2)}) collective-permute-start(bf16[512,256]{1,0:T(8,128)(2,1)} %constant_dynamic-update-slice_fusion), channel_id=1, source_target_pairs={{0,2},{1,3},{4,6},{5,7},{8,10},{9,11},{12,14},{13,15},{16,18},{17,... | collective-permute-start | bytes 786440 | tf_op jit(solution)/shard_map/ppermute | solution.py:24
  36.9 7.8 %copy-start.12 = (bf16[1,128,768]{2,1,0:T(8,128)(2,1)S(1)}, bf16[1,128,768]{2,1,0:T(8,128)(2,1)}, u32[]{:S(2)}) copy-start(bf16[1,128,768]{2,1,0:T(8,128)(2,1)} %param.6) | copy-start | bytes 589828
  40.2 17.0 %collective-permute-start = (bf16[512,256]{1,0:T(8,128)(2,1)}, bf16[512,256]{1,0:T(8,128)(2,1)S(1)}, u32[]{:S(2)}, u32[]{:S(2)}) collective-permute-start(bf16[512,256]{1,0:T(8,128)(2,1)} %constant_dynamic-update-slice_fusion), channel_id=1, source_target_pairs={{0,1},{1,2},{2,3},{4,5},{5,6},{6,7},{8,9},{9,10},{10,11},{12,13},{... | collective-permute-start | bytes 786440 | tf_op jit(solution)/shard_map/ppermute | solution.py:24
  45.4 7.7 %copy-start.11 = (bf16[8,128,768]{2,1,0:T(8,128)(2,1)S(1)}, bf16[8,128,768]{2,1,0:T(8,128)(2,1)}, u32[]{:S(2)}) copy-start(bf16[8,128,768]{2,1,0:T(8,128)(2,1)} %constant_dynamic-update-slice_fusion.2) | copy-start | bytes 4718596
  49.7 7.5 %copy-start.13 = (bf16[512,256]{1,0:T(8,128)(2,1)S(1)}, bf16[512,256]{1,0:T(8,128)(2,1)}, u32[]{:S(2)}) copy-start(bf16[512,256]{1,0:T(8,128)(2,1)} %constant_dynamic-update-slice_fusion) | copy-start | bytes 786436
  50.1 8.2 %collective-permute-start.12 = (bf16[512,2,4,128]{3,0,2,1:T(8,128)(2,1)S(1)}, bf16[512,2,4,128]{3,0,2,1:T(8,128)(2,1)S(1)}, u32[]{:S(2)}, u32[]{:S(2)}) collective-permute-start(bf16[512,2,4,128]{3,0,2,1:T(8,128)(2,1)S(1)} %bitcast.129), channel_id=1, source_target_pairs={{0,4},{4,0},{1,5},{5,1},{2,6},{6,2},{3,7},{7,3},{8,12},{12,8},{9,1... | collective-permute-start | bytes 3145736 | tf_op jit(solution)/shard_map/ppermute | solution.py:20
  54.1 27.4 %collective-permute-start.7 = (bf16[4,128,768]{2,1,0:T(8,128)(2,1)S(1)}, bf16[4,128,768]{2,1,0:T(8,128)(2,1)S(1)}, u32[]{:S(2)}, u32[]{:S(2)}) collective-permute-start(bf16[4,128,768]{2,1,0:T(8,128)(2,1)S(1)} %constant_dynamic-slice_fusion.2), channel_id=1, source_target_pairs={{0,128},{64,192},{128,0},{192,64},{1,129},{65,193},{129,1},{193,65... | collective-permute-start | bytes 2359304 | tf_op jit(solution)/shard_map/ppermute | solution.py:20
  54.3 5.9 %copy-start.14 = (bf16[512,128]{1,0:T(8,128)(2,1)S(1)}, bf16[512,128]{1,0:T(8,128)(2,1)}, u32[]{:S(2)}) copy-start(bf16[512,128]{1,0:T(8,128)(2,1)} %param.8) | copy-start | bytes 393220
  54.3 5.9 %copy-start.15 = (s32[512]{0:T(512)S(1)}, s32[512]{0:T(512)}, u32[]{:S(2)}) copy-start(s32[512]{0:T(512)} %iota_add_fusion) | copy-start | bytes 6148
  54.3 5.9 %copy-start.16 = (s32[512]{0:T(512)S(1)}, s32[512]{0:T(512)}, u32[]{:S(2)}) copy-start(s32[512]{0:T(512)} %convert_reduce_fusion.1) | copy-start | bytes 6148
  54.4 34.9 %collective-permute-start.6 = (bf16[4,128,768]{2,1,0:T(8,128)(2,1)S(1)}, bf16[4,128,768]{2,1,0:T(8,128)(2,1)S(1)}, u32[]{:S(2)}, u32[]{:S(2)}) collective-permute-start(bf16[4,128,768]{2,1,0:T(8,128)(2,1)S(1)} %constant_dynamic-slice_fusion.2), channel_id=1, source_target_pairs={{0,192},{64,0},{128,64},{192,128},{1,193},{65,1},{129,65},{193,129... | collective-permute-start | bytes 2359304 | tf_op jit(solution)/shard_map/ppermute | solution.py:20
  57.2 34.8 %collective-permute-start.8 = (bf16[4,128,768]{2,1,0:T(8,128)(2,1)S(1)}, bf16[4,128,768]{2,1,0:T(8,128)(2,1)S(1)}, u32[]{:S(2)}, u32[]{:S(2)}) collective-permute-start(bf16[4,128,768]{2,1,0:T(8,128)(2,1)S(1)} %constant_dynamic-slice_fusion.2), channel_id=1, source_target_pairs={{0,64},{64,128},{128,192},{192,0},{1,65},{65,129},{129,193},{193,1... | collective-permute-start | bytes 2359304 | tf_op jit(solution)/shard_map/ppermute | solution.py:20
  58.4 39.5 %copy-start.9 = (bf16[4,512,256]{2,1,0:T(8,128)(2,1)}, bf16[4,512,256]{2,1,0:T(8,128)(2,1)S(1)}, u32[]{:S(2)}) copy-start(bf16[4,512,256]{2,1,0:T(8,128)(2,1)S(1)} %pad_maximum_fusion.1) | copy-start | bytes 3145732
  58.9 8.6 %collective-permute-start.13 = (bf16[512,2,128]{2,0,1:T(8,128)(2,1)S(1)}, bf16[512,2,128]{2,0,1:T(8,128)(2,1)S(1)}, u32[]{:S(2)}, u32[]{:S(2)}) collective-permute-start(bf16[512,2,128]{2,0,1:T(8,128)(2,1)S(1)} %get-tuple-element.31), channel_id=1, source_target_pairs={{0,8},{8,16},{16,24},{24,0},{1,9},{9,17},{17,25},{25,1},{2,10},{10... | collective-permute-start | bytes 786440 | tf_op jit(solution)/shard_map/ppermute | solution.py:20
  61.3 9.5 %collective-permute-start.15 = (bf16[512,2,128]{2,0,1:T(8,128)(2,1)S(1)}, bf16[512,2,128]{2,0,1:T(8,128)(2,1)S(1)}, u32[]{:S(2)}, u32[]{:S(2)}) collective-permute-start(bf16[512,2,128]{2,0,1:T(8,128)(2,1)S(1)} %get-tuple-element.32), channel_id=1, source_target_pairs={{0,24},{8,0},{16,8},{24,16},{1,25},{9,1},{17,9},{25,17},{2,26},{10... | collective-permute-start | bytes 786440 | tf_op jit(solution)/shard_map/ppermute | solution.py:20
  67.5 7.9 %collective-permute-start.14 = (bf16[512,2,128]{2,0,1:T(8,128)(2,1)S(1)}, bf16[512,2,128]{2,0,1:T(8,128)(2,1)S(1)}, u32[]{:S(2)}, u32[]{:S(2)}) collective-permute-start(bf16[512,2,128]{2,0,1:T(8,128)(2,1)S(1)} %get-tuple-element.33), channel_id=1, source_target_pairs={{0,16},{8,24},{16,0},{24,8},{1,17},{9,25},{17,1},{25,9},{2,18},{10... | collective-permute-start | bytes 786440 | tf_op jit(solution)/shard_map/ppermute | solution.py:20
  75.5 16.9 %collective-permute-start.16 = (bf16[512,128]{1,0:T(8,128)(2,1)S(1)}, bf16[512,128]{1,0:T(8,128)(2,1)S(1)}, u32[]{:S(2)}, u32[]{:S(2)}) collective-permute-start(bf16[512,128]{1,0:T(8,128)(2,1)S(1)} %dynamic-slice_bitcast_fusion.3), channel_id=1, source_target_pairs={{0,32},{32,0},{1,33},{33,1},{2,34},{34,2},{3,35},{35,3},{4,36},{36... | collective-permute-start | bytes 393224 | tf_op jit(solution)/shard_map/ppermute | solution.py:20
  108.5 6.1 %copy-start.10 = (bf16[4,512,256]{2,1,0:T(8,128)(2,1)S(1)}, bf16[4,512,256]{2,1,0:T(8,128)(2,1)}, u32[]{:S(2)}) copy-start(bf16[4,512,256]{2,1,0:T(8,128)(2,1)} %copy-done.9) | copy-start | bytes 3145732
  108.6 12.4 %collective-permute-start.17 = (bf16[512,256]{0,1:T(8,128)(2,1)S(1)}, bf16[512,256]{0,1:T(8,128)(2,1)S(1)}, u32[]{:S(2)}, u32[]{:S(2)}) collective-permute-start(bf16[512,256]{0,1:T(8,128)(2,1)S(1)} %get-tuple-element.28), channel_id=1, source_target_pairs={{1,0},{2,1},{3,2},{5,4},{6,5},{7,6},{9,8},{10,9},{11,10},{13,12},{... | collective-permute-start | bytes 786440 | tf_op jit(solution)/shard_map/ppermute | solution.py:24
  110.0 14.8 %collective-permute-start.19 = (bf16[512,256]{0,1:T(8,128)(2,1)S(1)}, bf16[512,256]{0,1:T(8,128)(2,1)S(1)}, u32[]{:S(2)}, u32[]{:S(2)}) collective-permute-start(bf16[512,256]{0,1:T(8,128)(2,1)S(1)} %get-tuple-element.29), channel_id=1, source_target_pairs={{3,0},{7,4},{11,8},{15,12},{19,16},{23,20},{27,24},{31,28},{35,32}... | collective-permute-start | bytes 786440 | tf_op jit(solution)/shard_map/ppermute | solution.py:24
  111.3 25.9 %collective-permute-start.18 = (bf16[512,256]{0,1:T(8,128)(2,1)S(1)}, bf16[512,256]{0,1:T(8,128)(2,1)S(1)}, u32[]{:S(2)}, u32[]{:S(2)}) collective-permute-start(bf16[512,256]{0,1:T(8,128)(2,1)S(1)} %get-tuple-element.30), channel_id=1, source_target_pairs={{2,0},{3,1},{6,4},{7,5},{10,8},{11,9},{14,12},{15,13},{18,16},{19,... | collective-permute-start | bytes 786440 | tf_op jit(solution)/shard_map/ppermute | solution.py:24
  114.6 77.5 %copy-start.8 = (bf16[1,4,128,768]{3,2,0,1:T(8,128)(2,1)S(1)}, bf16[1,4,128,768]{3,2,0,1:T(8,128)(2,1)}, u32[]{:S(2)}) copy-start(bf16[1,4,128,768]{3,2,0,1:T(8,128)(2,1)} %get-tuple-element.23) | copy-start | bytes 2359300
  200.1 6.5 %copy-start.1 = (bf16[2048,768]{1,0:T(8,128)(2,1)S(1)}, bf16[2048,768]{1,0:T(8,128)(2,1)}, u32[]{:S(2)}) copy-start(bf16[2048,768]{1,0:T(8,128)(2,1)} %param.7) | copy-start | bytes 9437188
  (6 other events, 19.5 us)
Sparse Core Ops, SparseCore 0:
  101.9 90.2 all-gather.2
